TPU v7x, 32 devices: a whole 2x2x4 slice. The times are simulated.
32 devices in a mesh: grp: 4 (over z), shard: 8 (over y, x, core).
Axes of the slice: x: 2, y: 2, z: 4, core: 2. Of those that a mesh axis runs over, the one named last changes fastest.
Arguments:
- points: bfloat16 [65536, 768], P(('grp', 'shard')), may hold values from -6 to 6
- local_ids: int32 [65536], P(('grp', 'shard')), may hold values from 0 to 2047
- block_counts: int32 [32, 32], P(('grp', 'shard')), may hold values from 0 to 64, as said below
- centroids: float32 [65536, 768], P(('grp', 'shard')), may hold values from -6 to 6
- counts: float32 [65536], P(('grp', 'shard')), may hold values from 1 to 8
- queries: bfloat16 [1024, 768], P(('grp', 'shard')), may hold values from -6 to 6
Outputs:
- updated: float32 [65536, 768], P(('grp', 'shard'))
- new_counts: float32 [65536], P(('grp', 'shard'))
- distance: float32 [1024], P(('grp', 'shard'))
Inputs may be any that keep to these rules, and one draw needn't show every extreme that they name: block_counts[d, o] counts the occupied slots at the start of owner o's block in device d's buffer; the other slots of the block are padding whose points and ids matter to nothing. Some owner block is full in every device's buffer, and some owner receives full blocks from every device. `local_ids`: an index within the owning device's block of 2048 centroids.
All inputs are finite; a program needn't handle non-finite values.
Results may differ from a plain program's by a relative error of at most 0.0003.
Values may be sent and summed in bfloat16 or wider, within the bound.
No kernel may reach another device: no remote copies, remote signals or barrier semaphores. Data moves between devices by JAX's collectives and lax.ppermute only.
A program may use at most 128 MiB of HBM per device.

v0:
```python
import math

import jax
import jax.numpy as jnp
from jax import lax
from jax.sharding import PartitionSpec as P


def least_scores(query_rows, cent_rows):
    inner = lax.dot_general(
        query_rows, cent_rows, (((1,), (1,)), ((), ())), preferred_element_type=jnp.float32
    )
    cent_norm = jnp.sum(jnp.square(cent_rows.astype(jnp.float32)), axis=1)
    return jnp.min(cent_norm[None, :] - 2.0 * inner, axis=1)


def body(points, local_ids, block_counts, centroids, counts, queries):
    groups = lax.axis_size("grp")
    shards = lax.axis_size("shard")
    owners = groups * shards
    slot_rows, features = points.shape
    capacity = slot_rows // owners
    owned = centroids.shape[0]
    query_rows = queries.shape[0]
    position = lax.broadcasted_iota(jnp.int32, (owners, capacity), 1)
    filled = block_counts.reshape(owners, 1)
    tagged = jnp.where(position < filled, local_ids.reshape(owners, capacity), -1).reshape(
        slot_rows
    )
    arrived, arrived_ids = (
        lax.all_to_all(points, ("grp", "shard"), split_axis=0, concat_axis=0, tiled=True),
        lax.all_to_all(tagged, ("grp", "shard"), split_axis=0, concat_axis=0, tiled=True),
    )
    block_rows = math.gcd(512, slot_rows)
    block_count = slot_rows // block_rows
    centroid_index = lax.broadcasted_iota(jnp.int32, (1, owned), 1)

    def accumulate(totals, block_item):
        rows_part, ids_part = block_item
        onehot = (ids_part[:, None] == centroid_index).astype(jnp.bfloat16)
        sums_part = lax.dot_general(
            onehot, rows_part, (((0,), (0,)), ((), ())), preferred_element_type=jnp.float32
        )
        hits_part = jnp.sum(onehot.astype(jnp.float32), axis=0)
        return ((totals[0] + sums_part, totals[1] + hits_part), None)

    start_totals = (jnp.zeros((owned, features), jnp.float32), jnp.zeros((owned,), jnp.float32))
    (row_sums, hits), _ = lax.scan(
        accumulate,
        start_totals,
        (
            arrived.reshape(block_count, block_rows, features),
            arrived_ids.reshape(block_count, block_rows),
        ),
    )
    new_counts = counts + hits
    updated = centroids + (row_sums - hits[:, None] * centroids) / new_counts[:, None]
    rounded = updated.astype(jnp.bfloat16)
    query_norm = jnp.sum(jnp.square(queries.astype(jnp.float32)), axis=1)
    partial_min = least_scores(
        lax.all_gather(queries, ("grp", "shard"), axis=0, tiled=True), rounded
    )
    overall = lax.pmin(partial_min, ("grp", "shard"))
    own_best = lax.dynamic_slice_in_dim(
        overall, lax.axis_index(("grp", "shard")) * query_rows, query_rows
    )
    distance = (own_best + query_norm) / features
    return (updated, new_counts, distance)


def solution(mesh):
    placed = (
        P(("grp", "shard"), None),
        P(("grp", "shard")),
        P(("grp", "shard"), None),
        P(("grp", "shard"), None),
        P(("grp", "shard")),
        P(("grp", "shard"), None),
    )
    return jax.shard_map(
        body,
        mesh=mesh,
        in_specs=placed,
        out_specs=(P(("grp", "shard"), None), P(("grp", "shard")), P(("grp", "shard"))),
        check_vma=False,
    )
```

profile of v0, /device:TPU:0, one launch (start us, length us, event | category | flops | bytes accessed | tf_op | source)
XLA Modules:
  0.0 193.5 jit_solution(11400284474818124297)
XLA Ops:
  7.2 0.7 iota_compare_fusion.4
  7.9 0.1 lt.23
  8.0 0.7 broadcast_select_fusion
  8.7 0.1 all_to_all.12
  8.8 14.3 %all_to_all.18 = s32[32,64,1]{1,2,0:T(1,128)S(1)} all-to-all(s32[32,64,1]{1,2,0:T(1,128)S(1)} %all_to_all.12), channel_id=1, replica_groups=mesh['grp'=4,'shard'=8] {'grp','shard'}, dimensions={0} | all-to-all | bytes 16384 | tf_op jit(solution)/shard_map/all_to_all | solution.py:32
  23.1 2.8 %all-to-all-start.1 = ((bf16[32,64,768]{2,1,0:T(8,128)(2,1)}), bf16[32,64,768]{2,1,0:T(8,128)(2,1)S(1)}, u32[]{:S(2)}, u32[]{:S(2)}) async-start(bf16[32,64,768]{2,1,0:T(8,128)(2,1)} %bitcast.14), calls=%async_computation.1 | async-start | bytes 6291456 | tf_op jit(solution)/shard_map/all_to_all | solution.py:31
  25.9 0.7 all-gather.2.cloned.1.call-update
  26.7 0.1 multiply_reduce_fusion.1
  26.8 0.5 broadcast.26
  27.3 0.7 reduce.4
  28.1 76.6 %all-to-all-done.1 = bf16[32,64,768]{2,1,0:T(8,128)(2,1)S(1)} async-done(((bf16[32,64,768]{2,1,0:T(8,128)(2,1)}), bf16[32,64,768]{2,1,0:T(8,128)(2,1)S(1)}, u32[]{:S(2)}, u32[]{:S(2)}) %all-to-all-start.1) | async-done | bytes 3145760 | tf_op jit(solution)/shard_map/all_to_all | solution.py:31
  104.6 29.4 %while.13 = (s32[]{:T(128)}, f32[2048,768]{1,0:T(8,128)}, f32[2048]{0:T(1024)S(1)}, s32[4,512]{1,0:T(4,128)S(1)}, bf16[4,512,768]{2,1,0:T(8,128)(2,1)S(1)}, /*index=5*/s32[]{:T(128)}, s32[]{:T(128)}) while((s32[]{:T(128)}, f32[2048,768]{1,0:T(8,128)}, f32[2048]{0:T(1024)S(1)}, s32[4,512]{1,0:T(4,128)S(1)}, ...), condition=%wide.region_2.3_spmd.clone, body=%wide.region_0.2_spmd.clone.sunk | while | flops 1619003392 | bytes 13410400 | solution.py:48
  104.6 4.6 %select_add_fusion.4 = f32[2048,768]{1,0:T(8,128)} fusion(f32[2048,768]{1,0:T(8,128)} %get-tuple-element.109, pred[]{:T(512)S(6)} %compare.3, s32[512]{0:T(512)S(1)} %bitcast.15, bf16[4,512,768]{2,1,0:T(8,128)(2,1)S(1)} %get-tuple-element.119, s32[]{:T(128)} %get-tuple-element.108), kind=kOutput, calls=%fused_computation.1.clone.1 | convolution fusion | flops 1614807040 | bytes 13371397 | tf_op jit(solution)/shard_map/while/body/eval_jaxpr/dot_general | solution.py:41
  109.3 0.6 convert_reduce_fusion.2
  109.9 7.4 %select_add_fusion.4 = f32[2048,768]{1,0:T(8,128)} fusion(f32[2048,768]{1,0:T(8,128)} %get-tuple-element.109, pred[]{:T(512)S(6)} %compare.3, s32[512]{0:T(512)S(1)} %bitcast.15, bf16[4,512,768]{2,1,0:T(8,128)(2,1)S(1)} %get-tuple-element.119, s32[]{:T(128)} %get-tuple-element.108), kind=kOutput, calls=%fused_computation.1.clone.1 | convolution fusion | flops 1614807040 | bytes 13371397 | tf_op jit(solution)/shard_map/while/body/eval_jaxpr/dot_general | solution.py:41
  117.3 0.6 convert_reduce_fusion.2
  118.0 7.4 %select_add_fusion.4 = f32[2048,768]{1,0:T(8,128)} fusion(f32[2048,768]{1,0:T(8,128)} %get-tuple-element.109, pred[]{:T(512)S(6)} %compare.3, s32[512]{0:T(512)S(1)} %bitcast.15, bf16[4,512,768]{2,1,0:T(8,128)(2,1)S(1)} %get-tuple-element.119, s32[]{:T(128)} %get-tuple-element.108), kind=kOutput, calls=%fused_computation.1.clone.1 | convolution fusion | flops 1614807040 | bytes 13371397 | tf_op jit(solution)/shard_map/while/body/eval_jaxpr/dot_general | solution.py:41
  125.4 0.6 convert_reduce_fusion.2
  126.0 7.4 %select_add_fusion.4 = f32[2048,768]{1,0:T(8,128)} fusion(f32[2048,768]{1,0:T(8,128)} %get-tuple-element.109, pred[]{:T(512)S(6)} %compare.3, s32[512]{0:T(512)S(1)} %bitcast.15, bf16[4,512,768]{2,1,0:T(8,128)(2,1)S(1)} %get-tuple-element.119, s32[]{:T(128)} %get-tuple-element.108), kind=kOutput, calls=%fused_computation.1.clone.1 | convolution fusion | flops 1614807040 | bytes 13371397 | tf_op jit(solution)/shard_map/while/body/eval_jaxpr/dot_general | solution.py:41
  133.4 0.6 convert_reduce_fusion.2
  134.1 7.2 %multiply_reduce_fusion = (f32[2048]{0:T(1024)S(1)}, f32[2048,768]{1,0:T(8,128)}) fusion(f32[2048,768]{1,0:T(8,128)} %param.11, f32[2048]{0:T(1024)S(1)} %add.24, f32[2048,768]{1,0:T(8,128)} %get-tuple-element.36, f32[2048]{0:T(1024)S(1)} %get-tuple-element.37), kind=kLoop, calls=%fused_computation.13 | loop fusion | flops 12580864 | bytes 18898944 | tf_op jit(solution)/shard_map/reduce_sum | solution.py:13
  141.3 6.7 %subtract_reduce_fusion = f32[1024]{0:T(1024)S(1)} fusion(bf16[1024,768]{1,0:T(8,128)(2,1)} %all-gather.2.cloned.1.call-done, f32[2048]{0:T(1024)S(1)} %get-tuple-element.68, f32[2048,768]{1,0:T(8,128)} %get-tuple-element.69), kind=kOutput, calls=%fused_computation.12 | convolution fusion | flops 3229088768 | bytes 7876608 | tf_op jit(solution)/shard_map/dot_general | solution.py:10
  148.0 38.0 %pmin.7 = f32[1024]{0:T(1024)S(1)} all-reduce(f32[1024]{0:T(1024)S(1)} %subtract_reduce_fusion), channel_id=1, replica_groups=mesh['grp'=4,'shard'=8] {'grp','shard'}, use_global_device_ids=true, to_apply=%region_5.6 | all-reduce | flops 1024 | bytes 8192 | tf_op jit(solution)/shard_map/pmin | solution.py:63
  186.1 0.6 add_multiply_fusion
  (20 shorter events, 0.2 us)
Async XLA Ops:
  7.2 19.5 %copy-start = (bf16[32,768]{1,0:T(8,128)(2,1)S(1)}, bf16[32,768]{1,0:T(8,128)(2,1)}, u32[]{:S(2)}) copy-start(bf16[32,768]{1,0:T(8,128)(2,1)} %param.13) | copy-start | bytes 147460
  23.1 81.5 %all-to-all-start.1 = ((bf16[32,64,768]{2,1,0:T(8,128)(2,1)}), bf16[32,64,768]{2,1,0:T(8,128)(2,1)S(1)}, u32[]{:S(2)}, u32[]{:S(2)}) async-start(bf16[32,64,768]{2,1,0:T(8,128)(2,1)} %bitcast.14), calls=%async_computation.1 | async-start | bytes 6291456 | tf_op jit(solution)/shard_map/all_to_all | solution.py:31
  25.9 115.4 %all-gather.2.cloned.1.call-start = ((), (), s32[]{:S(2)}) async-start(), calls=%async_computation.2 | async-start | bytes 1622016 | tf_op jit(solution)/shard_map/all_gather | solution.py:61
  104.6 29.4 %copy-start.2 = (f32[2048]{0:T(1024)S(1)}, f32[2048]{0:T(1024)}, u32[]{:S(2)}) copy-start(f32[2048]{0:T(1024)} %param.12) | copy-start | bytes 24580
  134.1 7.2 %copy-start.1 = (f32[2048]{0:T(1024)}, f32[2048]{0:T(1024)S(1)}, u32[]{:S(2)}) copy-start(f32[2048]{0:T(1024)S(1)} %add.24) | copy-start | bytes 24580
Sparse Core Ops, SparseCore 0:
  29.6 65.6 all-gather.1
where the time goes:
time: 194 us; the launch traced here: 193 us
  waiting for transfers between devices  77.2 us (40%)
  blocking collectives  52.3 us (27%)
  matrix products  33.7 us (17%)
  between operations  14.1 us (7%)
  other arithmetic  12.3 us (6%)
  starting transfers between devices  2.82 us (1%)
    all_to_all x1, waiting for transfers between devices, body(): lax.all_to_all(points, ('grp', 'shard'), split_axis=0, concat_axis=0, til...  76.6 us
    pmin x1, blocking collectives, body(): overall = lax.pmin(partial_min, ('grp', 'shard'))  38 us
    dot_general x4, matrix products, accumulate(): lax.dot_general(onehot, rows_part, (((0,), (0,)), ((), ())), preferred_el...  26.9 us
    all_to_all x1, blocking collectives, body(): lax.all_to_all(tagged, ('grp', 'shard'), split_axis=0, concat_axis=0, til...  14.3 us
    reduce_sum x1, other arithmetic, least_scores(): cent_norm = jnp.sum(jnp.square(cent_rows.astype(jnp.float32)), axis=1)  7.22 us
    dot_general x1, matrix products, least_scores(): lax.dot_general(query_rows, cent_rows, (((1,), (1,)), ((), ())), preferre...  6.75 us
  transfers between devices with their start and end apart: 2, of which 1 were waited for; matrix products, arithmetic and copies ran while one was open for 20% of the time, Pallas kernels for 0%

commit v1 on v0

v1 whole, which is shorter than its diff:
```python
import functools

import jax
import jax.numpy as jnp
from jax import lax
from jax.experimental import pallas as pl
from jax.experimental.pallas import tpu as pltpu
from jax.sharding import PartitionSpec as P


def fused_kernel(ids_ref, rows_ref, cent_ref, counts_ref, q_ref, upd_ref, nc_ref, min_ref, *, tile):
    step = pl.program_id(0)
    centroid = step * tile + lax.broadcasted_iota(jnp.int32, (tile, 1), 0)
    match = ids_ref[...] == centroid
    onehot = jnp.where(match, 1.0, 0.0)
    sums = jnp.dot(
        onehot.astype(jnp.bfloat16), rows_ref[...], preferred_element_type=jnp.float32
    )
    hits = jnp.sum(onehot, axis=1, keepdims=True)
    cent = cent_ref[...]
    new_counts = counts_ref[...] + hits
    updated = cent + (sums - hits * cent) / new_counts
    upd_ref[...] = updated
    nc_ref[...] = new_counts
    rounded = updated.astype(jnp.bfloat16)
    wide = rounded.astype(jnp.float32)
    norm = jnp.sum(wide * wide, axis=1, keepdims=True)
    inner = lax.dot_general(
        rounded, q_ref[...], (((1,), (1,)), ((), ())), preferred_element_type=jnp.float32
    )
    least = jnp.min(norm - 2.0 * inner, axis=0, keepdims=True)

    @pl.when(step == 0)
    def _():
        min_ref[...] = least

    @pl.when(step > 0)
    def _():
        min_ref[...] = jnp.minimum(min_ref[...], least)


def fused_update(ids_row, rows, centroids, counts_col, all_queries, tile):
    owned, features = centroids.shape
    slots = rows.shape[0]
    query_all = all_queries.shape[0]
    steps = owned // tile
    flops = 2 * owned * slots * features + 2 * owned * query_all * features
    moved = rows.size * 2 + centroids.size * 8 + all_queries.size * 2
    return pl.pallas_call(
        functools.partial(fused_kernel, tile=tile),
        grid=(steps,),
        in_specs=[
            pl.BlockSpec((1, slots), lambda i: (0, 0)),
            pl.BlockSpec((slots, features), lambda i: (0, 0)),
            pl.BlockSpec((tile, features), lambda i: (i, 0)),
            pl.BlockSpec((tile, 1), lambda i: (i, 0)),
            pl.BlockSpec((query_all, features), lambda i: (0, 0)),
        ],
        out_specs=[
            pl.BlockSpec((tile, features), lambda i: (i, 0)),
            pl.BlockSpec((tile, 1), lambda i: (i, 0)),
            pl.BlockSpec((1, query_all), lambda i: (0, 0)),
        ],
        out_shape=[
            jax.ShapeDtypeStruct((owned, features), jnp.float32),
            jax.ShapeDtypeStruct((owned, 1), jnp.float32),
            jax.ShapeDtypeStruct((1, query_all), jnp.float32),
        ],
        compiler_params=pltpu.CompilerParams(
            dimension_semantics=("arbitrary",), vmem_limit_bytes=60 * 1024 * 1024
        ),
        cost_estimate=pl.CostEstimate(flops=flops, bytes_accessed=moved, transcendentals=0),
    )(ids_row, rows, centroids, counts_col, all_queries)


def body(points, local_ids, block_counts, centroids, counts, queries):
    groups = lax.axis_size("grp")
    shards = lax.axis_size("shard")
    owners = groups * shards
    slot_rows, features = points.shape
    capacity = slot_rows // owners
    owned = centroids.shape[0]
    query_rows = queries.shape[0]
    position = lax.broadcasted_iota(jnp.int32, (owners, capacity), 1)
    filled = block_counts.reshape(owners, 1)
    tagged = jnp.where(position < filled, local_ids.reshape(owners, capacity), -1).reshape(
        slot_rows
    )
    arrived = lax.all_to_all(points, ("grp", "shard"), split_axis=0, concat_axis=0, tiled=True)
    arrived_ids = lax.all_to_all(tagged, ("grp", "shard"), split_axis=0, concat_axis=0, tiled=True)
    all_queries = lax.all_gather(queries, ("grp", "shard"), axis=0, tiled=True)
    tile = 256 if owned % 256 == 0 else owned
    updated, new_counts, partial = fused_update(
        arrived_ids.reshape(1, slot_rows),
        arrived,
        centroids,
        counts.reshape(owned, 1),
        all_queries,
        tile,
    )
    gathered = lax.all_to_all(
        partial.reshape(owners, query_rows), ("grp", "shard"), split_axis=0, concat_axis=0,
        tiled=True,
    )
    own_best = jnp.min(gathered, axis=0)
    query_norm = jnp.sum(jnp.square(queries.astype(jnp.float32)), axis=1)
    distance = (own_best + query_norm) / features
    return (updated, new_counts.reshape(owned), distance)


def solution(mesh):
    placed = (
        P(("grp", "shard"), None),
        P(("grp", "shard")),
        P(("grp", "shard"), None),
        P(("grp", "shard"), None),
        P(("grp", "shard")),
        P(("grp", "shard"), None),
    )
    return jax.shard_map(
        body,
        mesh=mesh,
        in_specs=placed,
        out_specs=(P(("grp", "shard"), None), P(("grp", "shard")), P(("grp", "shard"))),
        check_vma=False,
    )
```

time: 194 us -> 146 us (0.75)
  blocking collectives: 52.3 us -> 14.3 us
  matrix products: 33.7 us -> 0 us
  Pallas kernels: 0 us -> 18.6 us
  other arithmetic: 12.3 us -> 6.32 us
  local copies, waits for them, and re-layouts: 0.81 us -> 5.58 us
  starting transfers between devices: 2.82 us -> 6.9 us
  waiting for transfers between devices: 77.2 us -> 80.3 us
    all_to_all x1, waiting for transfers between devices: 76.6 us -> 9.38 us  [body(): lax.all_to_all(points, ('grp', 'shard'), split_axis=0, concat_axis=0, til...]
    all_gather x1, waiting for transfers between devices: 0.01 us -> 65.4 us  [body(): all_queries = lax.all_gather(queries, ('grp', 'shard'), axis=0, tiled=True)]
    pmin x1 -> x0, blocking collectives: 38 us -> none  [body(): overall = lax.pmin(partial_min, ('grp', 'shard'))]
    dot_general x5 -> x0, matrix products: 33.7 us -> none  [the longest x4 26.9 us: accumulate(): lax.dot_general(onehot, rows_part, (((0,), (0,)), ((), ())), preferred_el...]
    pallas_call x0 -> x1, Pallas kernels: none -> 18.6 us  [fused_update(): pl.pallas_call(functools.partial(fused_kernel, tile=tile), grid=(steps,),...]
    reduce_sum x5 -> x0, other arithmetic: 9.47 us -> none  [the longest x1 7.22 us: least_scores(): cent_norm = jnp.sum(jnp.square(cent_rows.astype(jnp.float32)), axis=1)]
    all_to_all x0 -> x1, waiting for transfers between devices: none -> 4.87 us  [body(): lax.all_to_all(partial.reshape(owners, query_rows), ('grp', 'shard'), spl...]
    all_to_all x0 -> x1, starting transfers between devices: none -> 3.95 us  [body(): lax.all_to_all(partial.reshape(owners, query_rows), ('grp', 'shard'), spl...]
  transfers between devices with their start and end apart: 2 -> 3, of which waited for: 1 -> 3; matrix products, arithmetic and copies ran while one was open for 20% -> 4% of each run, Pallas kernels for 0% -> 0%
where the time goes in v1:
time: 146 us
  waiting for transfers between devices  80.3 us (55%)
  Pallas kernels  18.6 us (13%)
  blocking collectives  14.3 us (10%)
  between operations  14.1 us (10%)
  starting transfers between devices  6.9 us (5%)
  other arithmetic  6.32 us (4%)
  local copies, waits for them, and re-layouts  5.58 us (4%)
    all_gather x1, waiting for transfers between devices, body(): all_queries = lax.all_gather(queries, ('grp', 'shard'), axis=0, tiled=True)  65.4 us
    pallas_call x1, Pallas kernels, fused_update(): pl.pallas_call(functools.partial(fused_kernel, tile=tile), grid=(steps,),...  18.6 us
    all_to_all x1, blocking collectives, body(): lax.all_to_all(tagged, ('grp', 'shard'), split_axis=0, concat_axis=0, til...  14.3 us
    all_to_all x1, waiting for transfers between devices, body(): lax.all_to_all(points, ('grp', 'shard'), split_axis=0, concat_axis=0, til...  9.38 us
    all_to_all x1, waiting for transfers between devices, body(): lax.all_to_all(partial.reshape(owners, query_rows), ('grp', 'shard'), spl...  4.87 us
    all_to_all x1, starting transfers between devices, body(): lax.all_to_all(partial.reshape(owners, query_rows), ('grp', 'shard'), spl...  3.95 us
    pallas_call x2, other arithmetic, fused_update(): pl.pallas_call(functools.partial(fused_kernel, tile=tile), grid=(steps,),...  3.51 us
  transfers between devices with their start and end apart: 3, of which 3 were waited for; matrix products, arithmetic and copies ran while one was open for 4% of the time, Pallas kernels for 0%

profile of v1, /device:TPU:0, one launch (start us, length us, event | category | flops | bytes accessed | tf_op | source)
XLA Modules:
  0.0 146.1 jit_solution(14253078604737007175)
XLA Ops:
  7.2 0.7 iota_compare_fusion
  7.9 0.1 lt.17
  8.0 0.7 broadcast_select_fusion
  8.7 0.1 all_to_all.19
  8.8 14.3 %all_to_all.29 = s32[32,64,1]{1,2,0:T(1,128)S(1)} all-to-all(s32[32,64,1]{1,2,0:T(1,128)S(1)} %all_to_all.19), channel_id=1, replica_groups=mesh['grp'=4,'shard'=8] {'grp','shard'}, dimensions={0} | all-to-all | bytes 16384 | tf_op jit(solution)/shard_map/all_to_all | solution.py:90
  23.1 2.9 %all-to-all-start.1 = ((bf16[32,64,768]{2,1,0:T(8,128)(2,1)}), bf16[32,64,768]{2,1,0:T(8,128)(2,1)S(1)}, u32[]{:S(2)}, u32[]{:S(2)}) async-start(bf16[32,64,768]{2,1,0:T(8,128)(2,1)} %bitcast.6), calls=%async_computation.1 | async-start | bytes 6291456 | tf_op jit(solution)/shard_map/all_to_all | solution.py:89
  26.0 0.7 all-gather.2.cloned.1.call-update
  26.7 1.4 copy.10.counts_ref
  28.1 0.5 broadcast.12
  28.6 0.7 reduce.8
  29.3 0.7 reshape.31.ids_ref
  30.0 65.4 %all-gather.2.cloned.1.call-done.q_ref = bf16[1024,768]{1,0:T(8,128)(2,1)} async-done(((bf16[32,768]{1,0:T(8,128)(2,1)}), bf16[1024,768]{1,0:T(8,128)(2,1)}) %all-gather.2.cloned.1.call-update) | async-done | bytes 1572880 | tf_op jit(solution)/shard_map/all_gather | solution.py:91
  95.4 9.4 %all-to-all-done.1 = bf16[32,64,768]{2,1,0:T(8,128)(2,1)S(1)} async-done(((bf16[32,64,768]{2,1,0:T(8,128)(2,1)}), bf16[32,64,768]{2,1,0:T(8,128)(2,1)S(1)}, u32[]{:S(2)}, u32[]{:S(2)}) %all-to-all-start.1) | async-done | bytes 3145760 | tf_op jit(solution)/shard_map/all_to_all | solution.py:89
  104.7 1.7 %copy-done = bf16[32,64,768]{2,1,0:T(8,128)(2,1)} copy-done((bf16[32,64,768]{2,1,0:T(8,128)(2,1)}, bf16[32,64,768]{2,1,0:T(8,128)(2,1)S(1)}, u32[]{:S(2)}) %copy-start) | copy-done | bytes 3145752
  106.4 18.6 %shard_map.85 = (f32[2048,768]{1,0:T(8,128)}, f32[2048,1]{1,0:T(8,128)}, f32[1,1024]{1,0:T(1,128)}) custom-call(s32[1,2048]{1,0:T(1,128)} %reshape.31.ids_ref, bf16[2048,768]{1,0:T(8,128)(2,1)} %bitcast.7, f32[2048,768]{1,0:T(8,128)} %cent_ref.1, f32[2048,1]{1,0:T(8,128)} %copy.10.counts_ref, bf16[1024,768]{1,0:T(8,128)(2,1)} %all-gather.2.cloned.1.call-done.q_ref), custom_call_target="tpu_custom_call" | custom-call | flops 9663676416 | bytes 17301504 | tf_op jit(solution)/shard_map/pallas_call | solution.py:49
  125.0 0.5 broadcast.13
  125.5 1.3 reduce.9
  126.9 0.7 all_to_all.24
  127.6 3.9 %all-to-all-start.2 = ((f32[32,1,32]{2,1,0:T(1,128)}), f32[32,1,32]{2,1,0:T(1,128)S(1)}, u32[]{:S(2)}, u32[]{:S(2)}) async-start(f32[32,1,32]{2,1,0:T(1,128)} %bitcast.4), calls=%async_computation.2 | async-start | bytes 32768 | tf_op jit(solution)/shard_map/all_to_all | solution.py:101
  131.5 0.1 multiply_reduce_fusion
  131.6 2.2 %reduce.2 = f32[2048]{0:T(1024)} reduce(f32[2048,1]{1,0:T(8,128)} %get-tuple-element.7, f32[]{:T(128)} %constant.11), dimensions={1}, to_apply=%get-tuple-element.7.reduce_sub_computation | reduce | bytes 16388 | tf_op jit(solution)/shard_map/pallas_call | solution.py:49
  133.8 4.9 %all-to-all-done.2 = f32[32,1,32]{2,1,0:T(1,128)S(1)} async-done(((f32[32,1,32]{2,1,0:T(1,128)}), f32[32,1,32]{2,1,0:T(1,128)S(1)}, u32[]{:S(2)}, u32[]{:S(2)}) %all-to-all-start.2) | async-done | bytes 4128 | tf_op jit(solution)/shard_map/all_to_all | solution.py:101
  138.7 0.1 reduce_min.9
  138.7 0.5 add_multiply_fusion
  (6 shorter events, 0.1 us)
Async XLA Ops:
  23.1 3.7 %copy-start.2 = (f32[2048]{0:T(1024)S(1)}, f32[2048]{0:T(1024)}, u32[]{:S(2)}) copy-start(f32[2048]{0:T(1024)} %param.10) | copy-start | bytes 24580
  23.1 81.7 %all-to-all-start.1 = ((bf16[32,64,768]{2,1,0:T(8,128)(2,1)}), bf16[32,64,768]{2,1,0:T(8,128)(2,1)S(1)}, u32[]{:S(2)}, u32[]{:S(2)}) async-start(bf16[32,64,768]{2,1,0:T(8,128)(2,1)} %bitcast.6), calls=%async_computation.1 | async-start | bytes 6291456 | tf_op jit(solution)/shard_map/all_to_all | solution.py:89
  26.0 69.4 %all-gather.2.cloned.1.call-start = ((), (), s32[]{:S(2)}) async-start(), calls=%async_computation.3 | async-start | bytes 1622016 | tf_op jit(solution)/shard_map/all_gather | solution.py:91
  104.7 1.7 %copy-start = (bf16[32,64,768]{2,1,0:T(8,128)(2,1)}, bf16[32,64,768]{2,1,0:T(8,128)(2,1)S(1)}, u32[]{:S(2)}) copy-start(bf16[32,64,768]{2,1,0:T(8,128)(2,1)S(1)} %all-to-all-done.1) | copy-start | bytes 9437188
  106.4 25.1 %copy-start.1 = (bf16[32,768]{1,0:T(8,128)(2,1)S(1)}, bf16[32,768]{1,0:T(8,128)(2,1)}, u32[]{:S(2)}) copy-start(bf16[32,768]{1,0:T(8,128)(2,1)} %param.11) | copy-start | bytes 147460
  127.6 11.1 %all-to-all-start.2 = ((f32[32,1,32]{2,1,0:T(1,128)}), f32[32,1,32]{2,1,0:T(1,128)S(1)}, u32[]{:S(2)}, u32[]{:S(2)}) async-start(f32[32,1,32]{2,1,0:T(1,128)} %bitcast.4), calls=%async_computation.2 | async-start | bytes 32768 | tf_op jit(solution)/shard_map/all_to_all | solution.py:101
Sparse Core Ops, SparseCore 0:
  29.7 65.6 all-gather.1

commit v2 on v1

--- a/solution.py
+++ b/solution.py
@@ -87,7 +87,10 @@
         slot_rows
     )
     arrived = lax.all_to_all(points, ("grp", "shard"), split_axis=0, concat_axis=0, tiled=True)
-    arrived_ids = lax.all_to_all(tagged, ("grp", "shard"), split_axis=0, concat_axis=0, tiled=True)
+    every_ids = lax.all_gather(tagged.reshape(owners, capacity), ("grp", "shard"), axis=0)
+    arrived_ids = lax.dynamic_index_in_dim(
+        every_ids, lax.axis_index(("grp", "shard")), 1, keepdims=False
+    )
     all_queries = lax.all_gather(queries, ("grp", "shard"), axis=0, tiled=True)
     tile = 256 if owned % 256 == 0 else owned
     updated, new_counts, partial = fused_update(

time: 146 us -> 162 us (1.11)
  blocking collectives: 14.3 us -> 91.8 us
  waiting for transfers between devices: 80.3 us -> 5.56 us
  starting transfers between devices: 6.9 us -> 22.7 us
  other arithmetic: 6.32 us -> 4.27 us
    all_gather x0 -> x1, blocking collectives: none -> 91.8 us  [body(): lax.all_gather(tagged.reshape(owners, capacity), ('grp', 'shard'), axis=0)]
    all_gather x1, waiting for transfers between devices: 65.4 us -> 0.01 us  [body(): all_queries = lax.all_gather(queries, ('grp', 'shard'), axis=0, tiled=True)]
    all_to_all x1 -> x0, blocking collectives: 14.3 us -> none  [body(): lax.all_to_all(tagged, ('grp', 'shard'), split_axis=0, concat_axis=0, til...]
    all_to_all x1, starting transfers between devices: 3.95 us -> 15.4 us  [body(): lax.all_to_all(partial.reshape(owners, query_rows), ('grp', 'shard'), spl...]
    all_to_all x1, waiting for transfers between devices: 9.38 us -> 0.01 us  [body(): lax.all_to_all(points, ('grp', 'shard'), split_axis=0, concat_axis=0, til...]
    all_to_all x1, starting transfers between devices: 2.91 us -> 7.33 us  [body(): lax.all_to_all(points, ('grp', 'shard'), split_axis=0, concat_axis=0, til...]
  transfers between devices with their start and end apart: 3 -> 3, of which waited for: 3 -> 1; matrix products, arithmetic and copies ran while one was open for 4% -> 3% of each run, Pallas kernels for 0% -> 0%
where the time goes in v2:
time: 162 us
  blocking collectives  91.8 us (57%)
  starting transfers between devices  22.7 us (14%)
  Pallas kernels  18.6 us (11%)
  between operations  14.1 us (9%)
  waiting for transfers between devices  5.56 us (3%)
  local copies, waits for them, and re-layouts  5.03 us (3%)
  other arithmetic  4.27 us (3%)
    all_gather x1, blocking collectives, body(): lax.all_gather(tagged.reshape(owners, capacity), ('grp', 'shard'), axis=0)  91.8 us
    pallas_call x1, Pallas kernels, fused_update(): pl.pallas_call(functools.partial(fused_kernel, tile=tile), grid=(steps,),...  18.6 us
    all_to_all x1, starting transfers between devices, body(): lax.all_to_all(partial.reshape(owners, query_rows), ('grp', 'shard'), spl...  15.4 us
    all_to_all x1, starting transfers between devices, body(): lax.all_to_all(points, ('grp', 'shard'), split_axis=0, concat_axis=0, til...  7.33 us
    all_to_all x1, waiting for transfers between devices, body(): lax.all_to_all(partial.reshape(owners, query_rows), ('grp', 'shard'), spl...  4.87 us
    pallas_call x2, other arithmetic, fused_update(): pl.pallas_call(functools.partial(fused_kernel, tile=tile), grid=(steps,),...  3.51 us
  transfers between devices with their start and end apart: 3, of which 1 were waited for; matrix products, arithmetic and copies ran while one was open for 3% of the time, Pallas kernels for 0%

profile of v2, /device:TPU:0, one launch (start us, length us, event | category | flops | bytes accessed | tf_op | source)
XLA Modules:
  0.0 162.2 jit_solution(11779318136041598488)
XLA Ops:
  7.2 0.0 copy-start.3
  7.2 0.0 copy-start.4
  7.2 7.3 %all-to-all-start = ((bf16[32,64,768]{2,1,0:T(8,128)(2,1)}), bf16[32,64,768]{2,1,0:T(8,128)(2,1)S(1)}, u32[]{:S(2)}, u32[]{:S(2)}) async-start(bf16[32,64,768]{2,1,0:T(8,128)(2,1)} %bitcast.5), calls=%async_computation | async-start | bytes 6291456 | tf_op jit(solution)/shard_map/all_to_all | solution.py:89
  14.5 0.0 all-gather.2.cloned.1.call-start
  14.6 0.7 all-gather.2.cloned.1.call-update
  15.3 0.1 reshape.68
  15.4 0.1 fusion
  15.4 91.8 %all_gather.6 = s32[32,32,64]{2,1,0:T(8,128)S(1)} all-gather(s32[1,32,64]{2,1,0:T(8,128)S(1)} %fusion), channel_id=1, replica_groups=mesh['grp'=4,'shard'=8] {'grp','shard'}, dimensions={0}, use_global_device_ids=true | all-gather | bytes 270336 | tf_op jit(solution)/shard_map/all_gather | solution.py:90
  107.3 0.1 dynamic-slice_reduce_fusion
  107.3 0.7 reshape.69.ids_ref
  108.0 1.4 copy.10.counts_ref
  109.4 0.0 all-to-all-done
  109.4 1.7 %copy-done = bf16[32,64,768]{2,1,0:T(8,128)(2,1)} copy-done((bf16[32,64,768]{2,1,0:T(8,128)(2,1)}, bf16[32,64,768]{2,1,0:T(8,128)(2,1)S(1)}, u32[]{:S(2)}) %copy-start) | copy-done | bytes 3145752
  111.1 18.6 %shard_map.88 = (f32[2048,768]{1,0:T(8,128)}, f32[2048,1]{1,0:T(8,128)}, f32[1,1024]{1,0:T(1,128)}) custom-call(s32[1,2048]{1,0:T(1,128)} %reshape.69.ids_ref, bf16[2048,768]{1,0:T(8,128)(2,1)} %bitcast.6, f32[2048,768]{1,0:T(8,128)} %cent_ref.1, f32[2048,1]{1,0:T(8,128)} %copy.10.counts_ref, bf16[1024,768]{1,0:T(8,128)(2,1)} %all-gather.2.cloned.1.call-done.q_ref), custom_call_target="tpu_custom_call" | custom-call | flops 9663676416 | bytes 17301504 | tf_op jit(solution)/shard_map/pallas_call | solution.py:49
  129.7 0.5 broadcast.34
  130.2 1.3 reduce.9
  131.5 0.7 all_to_all.16
  132.2 15.4 %all-to-all-start.1 = ((f32[32,1,32]{2,1,0:T(1,128)}), f32[32,1,32]{2,1,0:T(1,128)S(1)}, u32[]{:S(2)}, u32[]{:S(2)}) async-start(f32[32,1,32]{2,1,0:T(1,128)} %bitcast.4), calls=%async_computation.1 | async-start | bytes 32768 | tf_op jit(solution)/shard_map/all_to_all | solution.py:104
  147.6 0.0 copy-done.1
  147.6 0.1 multiply_reduce_fusion
  147.7 2.2 %reduce.2 = f32[2048]{0:T(1024)} reduce(f32[2048,1]{1,0:T(8,128)} %get-tuple-element.7, f32[]{:T(128)} %constant.27), dimensions={1}, to_apply=%get-tuple-element.7.reduce_sub_computation | reduce | bytes 16388 | tf_op jit(solution)/shard_map/pallas_call | solution.py:49
  149.9 4.9 %all-to-all-done.1 = f32[32,1,32]{2,1,0:T(1,128)S(1)} async-done(((f32[32,1,32]{2,1,0:T(1,128)}), f32[32,1,32]{2,1,0:T(1,128)S(1)}, u32[]{:S(2)}, u32[]{:S(2)}) %all-to-all-start.1) | async-done | bytes 4128 | tf_op jit(solution)/shard_map/all_to_all | solution.py:104
  154.7 0.1 reduce_min.9
  154.8 0.5 add_multiply_fusion
  (7 shorter events, 0.0 us)
Async XLA Ops:
  7.2 8.1 %copy-start.3 = (s32[2048]{0:T(1024)S(1)}, s32[2048]{0:T(1024)}, u32[]{:S(2)}) copy-start(s32[2048]{0:T(1024)} %param.7) | copy-start | bytes 24580
  7.2 8.2 %copy-start.4 = (s32[1,32]{1,0:T(1,128)S(1)}, s32[1,32]{1,0:T(1,128)}, u32[]{:S(2)}) copy-start(s32[1,32]{1,0:T(1,128)} %param.8) | copy-start | bytes 388
  7.2 100.8 %copy-start.2 = (f32[2048]{0:T(1024)S(1)}, f32[2048]{0:T(1024)}, u32[]{:S(2)}) copy-start(f32[2048]{0:T(1024)} %param.10) | copy-start | bytes 24580
  7.2 102.2 %all-to-all-start = ((bf16[32,64,768]{2,1,0:T(8,128)(2,1)}), bf16[32,64,768]{2,1,0:T(8,128)(2,1)S(1)}, u32[]{:S(2)}, u32[]{:S(2)}) async-start(bf16[32,64,768]{2,1,0:T(8,128)(2,1)} %bitcast.5), calls=%async_computation | async-start | bytes 6291456 | tf_op jit(solution)/shard_map/all_to_all | solution.py:89
  14.5 94.9 %all-gather.2.cloned.1.call-start = ((), (), s32[]{:S(2)}) async-start(), calls=%async_computation.2 | async-start | bytes 1622016 | tf_op jit(solution)/shard_map/all_gather | solution.py:94
  109.4 1.7 %copy-start = (bf16[32,64,768]{2,1,0:T(8,128)(2,1)}, bf16[32,64,768]{2,1,0:T(8,128)(2,1)S(1)}, u32[]{:S(2)}) copy-start(bf16[32,64,768]{2,1,0:T(8,128)(2,1)S(1)} %all-to-all-done) | copy-start | bytes 9437188
  111.1 36.5 %copy-start.1 = (bf16[32,768]{1,0:T(8,128)(2,1)S(1)}, bf16[32,768]{1,0:T(8,128)(2,1)}, u32[]{:S(2)}) copy-start(bf16[32,768]{1,0:T(8,128)(2,1)} %param.11) | copy-start | bytes 147460
  132.2 22.5 %all-to-all-start.1 = ((f32[32,1,32]{2,1,0:T(1,128)}), f32[32,1,32]{2,1,0:T(1,128)S(1)}, u32[]{:S(2)}, u32[]{:S(2)}) async-start(f32[32,1,32]{2,1,0:T(1,128)} %bitcast.4), calls=%async_computation.1 | async-start | bytes 32768 | tf_op jit(solution)/shard_map/all_to_all | solution.py:104
Sparse Core Ops, SparseCore 0:
  18.2 65.4 all-gather.1

commit v3 on v1

--- a/solution.py
+++ b/solution.py
@@ -87,8 +87,18 @@
         slot_rows
     )
     arrived = lax.all_to_all(points, ("grp", "shard"), split_axis=0, concat_axis=0, tiled=True)
-    arrived_ids = lax.all_to_all(tagged, ("grp", "shard"), split_axis=0, concat_axis=0, tiled=True)
-    all_queries = lax.all_gather(queries, ("grp", "shard"), axis=0, tiled=True)
+    shifted = tagged + 1
+    codes = jnp.concatenate([shifted // 64, shifted % 64]).astype(jnp.bfloat16)
+    code_rows = -(-codes.shape[0] // features)
+    codes = jnp.pad(codes, (0, code_rows * features - codes.shape[0]))
+    payload = jnp.concatenate([queries, codes.reshape(code_rows, features)], axis=0)
+    gathered = lax.all_gather(payload, ("grp", "shard"), axis=0)
+    all_queries = gathered[:, :query_rows].reshape(owners * query_rows, features)
+    received = gathered[:, query_rows:].reshape(owners, code_rows * features)[:, : 2 * slot_rows]
+    received = received.reshape(owners, 2, owners, capacity)
+    mine = lax.dynamic_index_in_dim(received, lax.axis_index(("grp", "shard")), 2, keepdims=False)
+    mine = mine.astype(jnp.int32)
+    arrived_ids = mine[:, 0] * 64 + mine[:, 1] - 1
     tile = 256 if owned % 256 == 0 else owned
     updated, new_counts, partial = fused_update(
         arrived_ids.reshape(1, slot_rows),

time: 146 us -> 137 us (0.938)
  blocking collectives: 14.3 us -> 0 us
  starting transfers between devices: 6.9 us -> 11.6 us
  local copies, waits for them, and re-layouts: 5.58 us -> 10.1 us
  waiting for transfers between devices: 80.3 us -> 76.1 us
    all_to_all x1 -> x0, blocking collectives: 14.3 us -> none  [body(): lax.all_to_all(tagged, ('grp', 'shard'), split_axis=0, concat_axis=0, til...]
    all_to_all x1, waiting for transfers between devices: 9.38 us -> 2.79 us  [body(): lax.all_to_all(points, ('grp', 'shard'), split_axis=0, concat_axis=0, til...]
    all_to_all x1, starting transfers between devices: 2.91 us -> 7.33 us  [body(): lax.all_to_all(points, ('grp', 'shard'), split_axis=0, concat_axis=0, til...]
    slice x0 -> x3, local copies, waits for them, and re-layouts: none -> 3.69 us  [the longest x1 2.65 us: body(): gathered[:, :query_rows].reshape(owners * query_rows, features)]
    all_gather x1, waiting for transfers between devices: 65.4 us -> 68.4 us  [body(): gathered = lax.all_gather(payload, ('grp', 'shard'), axis=0)]
  transfers between devices with their start and end apart: 3 -> 3, of which waited for: 3 -> 3; matrix products, arithmetic and copies ran while one was open for 4% -> 8% of each run, Pallas kernels for 0% -> 0%
where the time goes in v3:
time: 137 us
  waiting for transfers between devices  76.1 us (56%)
  Pallas kernels  18.6 us (14%)
  between operations  14.2 us (10%)
  starting transfers between devices  11.6 us (8%)
  local copies, waits for them, and re-layouts  10.1 us (7%)
  other arithmetic  5.94 us (4%)
    all_gather x1, waiting for transfers between devices, body(): gathered = lax.all_gather(payload, ('grp', 'shard'), axis=0)  68.4 us
    pallas_call x1, Pallas kernels, fused_update(): pl.pallas_call(functools.partial(fused_kernel, tile=tile), grid=(steps,),...  18.6 us
    all_to_all x1, starting transfers between devices, body(): lax.all_to_all(points, ('grp', 'shard'), split_axis=0, concat_axis=0, til...  7.33 us
    all_to_all x1, waiting for transfers between devices, body(): lax.all_to_all(partial.reshape(owners, query_rows), ('grp', 'shard'), spl...  4.88 us
    all_to_all x1, starting transfers between devices, body(): lax.all_to_all(partial.reshape(owners, query_rows), ('grp', 'shard'), spl...  4.18 us
    pallas_call x2, other arithmetic, fused_update(): pl.pallas_call(functools.partial(fused_kernel, tile=tile), grid=(steps,),...  3.51 us
    all_to_all x1, waiting for transfers between devices, body(): lax.all_to_all(points, ('grp', 'shard'), split_axis=0, concat_axis=0, til...  2.79 us
  transfers between devices with their start and end apart: 3, of which 3 were waited for; matrix products, arithmetic and copies ran while one was open for 8% of the time, Pallas kernels for 0%

profile of v3, /device:TPU:0, one launch (start us, length us, event | category | flops | bytes accessed | tf_op | source)
XLA Modules:
  0.0 136.5 jit_solution(6257969315176962710)
XLA Ops:
  7.2 7.3 %all-to-all-start = ((bf16[32,64,768]{2,1,0:T(8,128)(2,1)}), bf16[32,64,768]{2,1,0:T(8,128)(2,1)S(1)}, u32[]{:S(2)}, u32[]{:S(2)}) async-start(bf16[32,64,768]{2,1,0:T(8,128)(2,1)} %bitcast.11), calls=%async_computation | async-start | bytes 6291456 | tf_op jit(solution)/shard_map/all_to_all | solution.py:89
  14.6 0.1 iota_compare_fusion.1
  14.7 0.1 lt.27
  14.8 0.6 maximum_bitcast_fusion
  15.5 1.4 %copy.10.counts_ref = f32[2048,1]{1,0:T(8,128)} copy(f32[2048,1]{0,1:T(1,128)S(1)} %bitcast.17) | data formatting | bytes 16384 | tf_op jit(solution)/shard_map/reshape | solution.py:107
  16.9 68.4 %all-gather.4.cloned.1.call-done = bf16[32,38,768]{2,1,0:T(8,128)(2,1)} async-done(((bf16[1,38,768]{2,1,0:T(8,128)(2,1)}), bf16[32,38,768]{2,1,0:T(8,128)(2,1)}) %all-gather.4.cloned.1.call-update) | async-done | bytes 1867792 | tf_op jit(solution)/shard_map/all_gather | solution.py:95
  85.4 1.0 slice.20
  86.4 0.1 copy.12
  86.5 1.3 reshape.70
  87.8 0.9 dynamic-slice_convert_fusion
  88.8 0.1 fusion.3
  88.8 0.7 sub.14.ids_ref
  89.5 2.6 %slice.24 = bf16[32,32,768]{2,1,0:T(8,128)(2,1)} slice(bf16[32,38,768]{2,1,0:T(8,128)(2,1)} %all-gather.4.cloned.1.call-done), slice={[0:32], [0:32], [0:768]} | slice | bytes 3145728 | tf_op jit(solution)/shard_map/slice | solution.py:96
  92.2 2.8 %all-to-all-done = bf16[32,64,768]{2,1,0:T(8,128)(2,1)S(1)} async-done(((bf16[32,64,768]{2,1,0:T(8,128)(2,1)}), bf16[32,64,768]{2,1,0:T(8,128)(2,1)S(1)}, u32[]{:S(2)}, u32[]{:S(2)}) %all-to-all-start) | async-done | bytes 3145760 | tf_op jit(solution)/shard_map/all_to_all | solution.py:89
  95.0 1.7 %copy-done = bf16[32,64,768]{2,1,0:T(8,128)(2,1)} copy-done((bf16[32,64,768]{2,1,0:T(8,128)(2,1)}, bf16[32,64,768]{2,1,0:T(8,128)(2,1)S(1)}, u32[]{:S(2)}) %copy-start) | copy-done | bytes 3145752
  96.6 18.6 %shard_map.85 = (f32[2048,768]{1,0:T(8,128)}, f32[2048,1]{1,0:T(8,128)}, f32[1,1024]{1,0:T(1,128)}) custom-call(s32[1,2048]{1,0:T(1,128)} %sub.14.ids_ref, bf16[2048,768]{1,0:T(8,128)(2,1)} %bitcast.12, f32[2048,768]{1,0:T(8,128)} %cent_ref.1, f32[2048,1]{1,0:T(8,128)} %copy.10.counts_ref, bf16[1024,768]{1,0:T(8,128)(2,1)} %bitcast.13), custom_call_target="tpu_custom_call" | custom-call | flops 9663676416 | bytes 17301504 | tf_op jit(solution)/shard_map/pallas_call | solution.py:49
  115.2 0.5 broadcast.67
  115.7 1.3 reduce.9
  117.1 0.7 all_to_all.16
  117.7 4.2 %all-to-all-start.1 = ((f32[32,1,32]{2,1,0:T(1,128)}), f32[32,1,32]{2,1,0:T(1,128)S(1)}, u32[]{:S(2)}, u32[]{:S(2)}) async-start(f32[32,1,32]{2,1,0:T(1,128)} %bitcast.7), calls=%async_computation.1 | async-start | bytes 32768 | tf_op jit(solution)/shard_map/all_to_all | solution.py:111
  121.9 0.1 multiply_reduce_fusion
  122.0 2.2 %reduce.2 = f32[2048]{0:T(1024)} reduce(f32[2048,1]{1,0:T(8,128)} %get-tuple-element.7, f32[]{:T(128)} %constant.62), dimensions={1}, to_apply=%get-tuple-element.7.reduce_sub_computation | reduce | bytes 16388 | tf_op jit(solution)/shard_map/pallas_call | solution.py:49
  124.2 4.9 %all-to-all-done.1 = f32[32,1,32]{2,1,0:T(1,128)S(1)} async-done(((f32[32,1,32]{2,1,0:T(1,128)}), f32[32,1,32]{2,1,0:T(1,128)S(1)}, u32[]{:S(2)}, u32[]{:S(2)}) %all-to-all-start.1) | async-done | bytes 4128 | tf_op jit(solution)/shard_map/all_to_all | solution.py:111
  129.2 0.5 add_multiply_fusion
  (16 shorter events, 0.2 us)
Async XLA Ops:
  7.2 7.4 %copy-start.4 = (s32[1,32]{1,0:T(1,128)S(1)}, s32[1,32]{1,0:T(1,128)}, u32[]{:S(2)}) copy-start(s32[1,32]{1,0:T(1,128)} %param.8) | copy-start | bytes 388
  7.2 7.6 %copy-start.3 = (s32[2048]{0:T(1024)S(1)}, s32[2048]{0:T(1024)}, u32[]{:S(2)}) copy-start(s32[2048]{0:T(1024)} %param.7) | copy-start | bytes 24580
  7.2 7.7 %copy-start.1 = (bf16[32,768]{1,0:T(8,128)(2,1)S(1)}, bf16[32,768]{1,0:T(8,128)(2,1)}, u32[]{:S(2)}) copy-start(bf16[32,768]{1,0:T(8,128)(2,1)} %param.11) | copy-start | bytes 147460
  7.2 8.3 %copy-start.2 = (f32[2048]{0:T(1024)S(1)}, f32[2048]{0:T(1024)}, u32[]{:S(2)}) copy-start(f32[2048]{0:T(1024)} %param.10) | copy-start | bytes 24580
  7.2 87.7 %all-to-all-start = ((bf16[32,64,768]{2,1,0:T(8,128)(2,1)}), bf16[32,64,768]{2,1,0:T(8,128)(2,1)S(1)}, u32[]{:S(2)}, u32[]{:S(2)}) async-start(bf16[32,64,768]{2,1,0:T(8,128)(2,1)} %bitcast.11), calls=%async_computation | async-start | bytes 6291456 | tf_op jit(solution)/shard_map/all_to_all | solution.py:89
  14.5 70.8 %all-gather.4.cloned.1.call-start = ((), (), s32[]{:S(2)}) async-start(), calls=%async_computation.2 | async-start | bytes 2027520 | tf_op jit(solution)/shard_map/all_gather | solution.py:95
  95.0 1.7 %copy-start = (bf16[32,64,768]{2,1,0:T(8,128)(2,1)}, bf16[32,64,768]{2,1,0:T(8,128)(2,1)S(1)}, u32[]{:S(2)}) copy-start(bf16[32,64,768]{2,1,0:T(8,128)(2,1)S(1)} %all-to-all-done) | copy-start | bytes 9437188
  117.7 11.4 %all-to-all-start.1 = ((f32[32,1,32]{2,1,0:T(1,128)}), f32[32,1,32]{2,1,0:T(1,128)S(1)}, u32[]{:S(2)}, u32[]{:S(2)}) async-start(f32[32,1,32]{2,1,0:T(1,128)} %bitcast.7), calls=%async_computation.1 | async-start | bytes 32768 | tf_op jit(solution)/shard_map/all_to_all | solution.py:111
Sparse Core Ops, SparseCore 0:
  18.8 66.4 all-gather.3

commit v4 on v3

--- a/solution.py
+++ b/solution.py
@@ -99,7 +99,7 @@
     mine = lax.dynamic_index_in_dim(received, lax.axis_index(("grp", "shard")), 2, keepdims=False)
     mine = mine.astype(jnp.int32)
     arrived_ids = mine[:, 0] * 64 + mine[:, 1] - 1
-    tile = 256 if owned % 256 == 0 else owned
+    tile = 512 if owned % 512 == 0 else owned
     updated, new_counts, partial = fused_update(
         arrived_ids.reshape(1, slot_rows),
         arrived,

time: 137 us -> 136 us (level)
  no operation moved by 1% of the time
where the time goes in v4:
time: 136 us; the launch traced here: 135 us
  waiting for transfers between devices  76.1 us (56%)
  Pallas kernels  17.3 us (13%)
  between operations  14.2 us (10%)
  starting transfers between devices  11.5 us (8%)
  local copies, waits for them, and re-layouts  10.1 us (7%)
  other arithmetic  5.94 us (4%)
    all_gather x1, waiting for transfers between devices, body(): gathered = lax.all_gather(payload, ('grp', 'shard'), axis=0)  68.4 us
    pallas_call x1, Pallas kernels, fused_update(): pl.pallas_call(functools.partial(fused_kernel, tile=tile), grid=(steps,),...  17.3 us
    all_to_all x1, starting transfers between devices, body(): lax.all_to_all(points, ('grp', 'shard'), split_axis=0, concat_axis=0, til...  7.33 us
    all_to_all x1, waiting for transfers between devices, body(): lax.all_to_all(partial.reshape(owners, query_rows), ('grp', 'shard'), spl...  4.88 us
    all_to_all x1, starting transfers between devices, body(): lax.all_to_all(partial.reshape(owners, query_rows), ('grp', 'shard'), spl...  4.16 us
    pallas_call x2, other arithmetic, fused_update(): pl.pallas_call(functools.partial(fused_kernel, tile=tile), grid=(steps,),...  3.51 us
    all_to_all x1, waiting for transfers between devices, body(): lax.all_to_all(points, ('grp', 'shard'), split_axis=0, concat_axis=0, til...  2.79 us
  transfers between devices with their start and end apart: 3, of which 3 were waited for; matrix products, arithmetic and copies ran while one was open for 8% of the time, Pallas kernels for 0%

profile of v4, /device:TPU:0, one launch (start us, length us, event | category | flops | bytes accessed | tf_op | source)
XLA Modules:
  0.0 135.2 jit_solution(11620049371693642192)
XLA Ops:
  7.2 7.3 %all-to-all-start = ((bf16[32,64,768]{2,1,0:T(8,128)(2,1)}), bf16[32,64,768]{2,1,0:T(8,128)(2,1)S(1)}, u32[]{:S(2)}, u32[]{:S(2)}) async-start(bf16[32,64,768]{2,1,0:T(8,128)(2,1)} %bitcast.11), calls=%async_computation | async-start | bytes 6291456 | tf_op jit(solution)/shard_map/all_to_all | solution.py:89
  14.6 0.1 iota_compare_fusion.1
  14.7 0.1 lt.27
  14.8 0.6 maximum_bitcast_fusion
  15.5 1.4 %copy.10.counts_ref = f32[2048,1]{1,0:T(8,128)} copy(f32[2048,1]{0,1:T(1,128)S(1)} %bitcast.17) | data formatting | bytes 16384 | tf_op jit(solution)/shard_map/reshape | solution.py:107
  16.9 68.4 %all-gather.4.cloned.1.call-done = bf16[32,38,768]{2,1,0:T(8,128)(2,1)} async-done(((bf16[1,38,768]{2,1,0:T(8,128)(2,1)}), bf16[32,38,768]{2,1,0:T(8,128)(2,1)}) %all-gather.4.cloned.1.call-update) | async-done | bytes 1867792 | tf_op jit(solution)/shard_map/all_gather | solution.py:95
  85.4 1.0 slice.20
  86.4 0.1 copy.12
  86.5 1.3 reshape.70
  87.8 0.9 dynamic-slice_convert_fusion
  88.8 0.1 fusion.3
  88.8 0.7 sub.14.ids_ref
  89.5 2.6 %slice.24 = bf16[32,32,768]{2,1,0:T(8,128)(2,1)} slice(bf16[32,38,768]{2,1,0:T(8,128)(2,1)} %all-gather.4.cloned.1.call-done), slice={[0:32], [0:32], [0:768]} | slice | bytes 3145728 | tf_op jit(solution)/shard_map/slice | solution.py:96
  92.2 2.8 %all-to-all-done = bf16[32,64,768]{2,1,0:T(8,128)(2,1)S(1)} async-done(((bf16[32,64,768]{2,1,0:T(8,128)(2,1)}), bf16[32,64,768]{2,1,0:T(8,128)(2,1)S(1)}, u32[]{:S(2)}, u32[]{:S(2)}) %all-to-all-start) | async-done | bytes 3145760 | tf_op jit(solution)/shard_map/all_to_all | solution.py:89
  95.0 1.7 %copy-done = bf16[32,64,768]{2,1,0:T(8,128)(2,1)} copy-done((bf16[32,64,768]{2,1,0:T(8,128)(2,1)}, bf16[32,64,768]{2,1,0:T(8,128)(2,1)S(1)}, u32[]{:S(2)}) %copy-start) | copy-done | bytes 3145752
  96.6 17.3 %shard_map.85 = (f32[2048,768]{1,0:T(8,128)}, f32[2048,1]{1,0:T(8,128)}, f32[1,1024]{1,0:T(1,128)}) custom-call(s32[1,2048]{1,0:T(1,128)} %sub.14.ids_ref, bf16[2048,768]{1,0:T(8,128)(2,1)} %bitcast.12, f32[2048,768]{1,0:T(8,128)} %cent_ref.1, f32[2048,1]{1,0:T(8,128)} %copy.10.counts_ref, bf16[1024,768]{1,0:T(8,128)(2,1)} %bitcast.13), custom_call_target="tpu_custom_call" | custom-call | flops 9663676416 | bytes 17301504 | tf_op jit(solution)/shard_map/pallas_call | solution.py:49
  113.9 0.5 broadcast.67
  114.4 1.3 reduce.9
  115.7 0.7 all_to_all.16
  116.4 4.2 %all-to-all-start.1 = ((f32[32,1,32]{2,1,0:T(1,128)}), f32[32,1,32]{2,1,0:T(1,128)S(1)}, u32[]{:S(2)}, u32[]{:S(2)}) async-start(f32[32,1,32]{2,1,0:T(1,128)} %bitcast.7), calls=%async_computation.1 | async-start | bytes 32768 | tf_op jit(solution)/shard_map/all_to_all | solution.py:111
  120.6 0.1 multiply_reduce_fusion
  120.7 2.2 %reduce.2 = f32[2048]{0:T(1024)} reduce(f32[2048,1]{1,0:T(8,128)} %get-tuple-element.7, f32[]{:T(128)} %constant.62), dimensions={1}, to_apply=%get-tuple-element.7.reduce_sub_computation | reduce | bytes 16388 | tf_op jit(solution)/shard_map/pallas_call | solution.py:49
  122.9 4.9 %all-to-all-done.1 = f32[32,1,32]{2,1,0:T(1,128)S(1)} async-done(((f32[32,1,32]{2,1,0:T(1,128)}), f32[32,1,32]{2,1,0:T(1,128)S(1)}, u32[]{:S(2)}, u32[]{:S(2)}) %all-to-all-start.1) | async-done | bytes 4128 | tf_op jit(solution)/shard_map/all_to_all | solution.py:111
  127.8 0.5 add_multiply_fusion
  (16 shorter events, 0.2 us)
Async XLA Ops:
  7.2 7.4 %copy-start.4 = (s32[1,32]{1,0:T(1,128)S(1)}, s32[1,32]{1,0:T(1,128)}, u32[]{:S(2)}) copy-start(s32[1,32]{1,0:T(1,128)} %param.8) | copy-start | bytes 388
  7.2 7.6 %copy-start.3 = (s32[2048]{0:T(1024)S(1)}, s32[2048]{0:T(1024)}, u32[]{:S(2)}) copy-start(s32[2048]{0:T(1024)} %param.7) | copy-start | bytes 24580
  7.2 7.7 %copy-start.1 = (bf16[32,768]{1,0:T(8,128)(2,1)S(1)}, bf16[32,768]{1,0:T(8,128)(2,1)}, u32[]{:S(2)}) copy-start(bf16[32,768]{1,0:T(8,128)(2,1)} %param.11) | copy-start | bytes 147460
  7.2 8.3 %copy-start.2 = (f32[2048]{0:T(1024)S(1)}, f32[2048]{0:T(1024)}, u32[]{:S(2)}) copy-start(f32[2048]{0:T(1024)} %param.10) | copy-start | bytes 24580
  7.2 87.7 %all-to-all-start = ((bf16[32,64,768]{2,1,0:T(8,128)(2,1)}), bf16[32,64,768]{2,1,0:T(8,128)(2,1)S(1)}, u32[]{:S(2)}, u32[]{:S(2)}) async-start(bf16[32,64,768]{2,1,0:T(8,128)(2,1)} %bitcast.11), calls=%async_computation | async-start | bytes 6291456 | tf_op jit(solution)/shard_map/all_to_all | solution.py:89
  14.5 70.8 %all-gather.4.cloned.1.call-start = ((), (), s32[]{:S(2)}) async-start(), calls=%async_computation.2 | async-start | bytes 2027520 | tf_op jit(solution)/shard_map/all_gather | solution.py:95
  95.0 1.7 %copy-start = (bf16[32,64,768]{2,1,0:T(8,128)(2,1)}, bf16[32,64,768]{2,1,0:T(8,128)(2,1)S(1)}, u32[]{:S(2)}) copy-start(bf16[32,64,768]{2,1,0:T(8,128)(2,1)S(1)} %all-to-all-done) | copy-start | bytes 9437188
  116.4 11.3 %all-to-all-start.1 = ((f32[32,1,32]{2,1,0:T(1,128)}), f32[32,1,32]{2,1,0:T(1,128)S(1)}, u32[]{:S(2)}, u32[]{:S(2)}) async-start(f32[32,1,32]{2,1,0:T(1,128)} %bitcast.7), calls=%async_computation.1 | async-start | bytes 32768 | tf_op jit(solution)/shard_map/all_to_all | solution.py:111
Sparse Core Ops, SparseCore 0:
  18.8 66.4 all-gather.3

commit v5 on v4

--- a/solution.py
+++ b/solution.py
@@ -8,7 +8,7 @@
 from jax.sharding import PartitionSpec as P
 
 
-def fused_kernel(ids_ref, rows_ref, cent_ref, counts_ref, q_ref, upd_ref, nc_ref, min_ref, *, tile):
+def fused_kernel(ids_ref, rows_ref, cent_ref, counts_ref, q_ref, upd_ref, nc_ref, min_ref, run_ref, *, tile):
     step = pl.program_id(0)
     centroid = step * tile + lax.broadcasted_iota(jnp.int32, (tile, 1), 0)
     match = ids_ref[...] == centroid
@@ -32,14 +32,20 @@
 
     @pl.when(step == 0)
     def _():
-        min_ref[...] = least
+        run_ref[...] = least
 
     @pl.when(step > 0)
     def _():
-        min_ref[...] = jnp.minimum(min_ref[...], least)
+        run_ref[...] = jnp.minimum(run_ref[...], least)
+
+    @pl.when(step == pl.num_programs(0) - 1)
+    def _():
+        owners, _, query_rows = min_ref.shape
+        for owner in range(owners):
+            min_ref[owner] = run_ref[:, owner * query_rows : (owner + 1) * query_rows]
 
 
-def fused_update(ids_row, rows, centroids, counts_col, all_queries, tile):
+def fused_update(ids_row, rows, centroids, counts_col, all_queries, tile, owners):
     owned, features = centroids.shape
     slots = rows.shape[0]
     query_all = all_queries.shape[0]
@@ -59,13 +65,14 @@
         out_specs=[
             pl.BlockSpec((tile, features), lambda i: (i, 0)),
             pl.BlockSpec((tile, 1), lambda i: (i, 0)),
-            pl.BlockSpec((1, query_all), lambda i: (0, 0)),
+            pl.BlockSpec((owners, 1, query_all // owners), lambda i: (0, 0, 0)),
         ],
         out_shape=[
             jax.ShapeDtypeStruct((owned, features), jnp.float32),
             jax.ShapeDtypeStruct((owned, 1), jnp.float32),
-            jax.ShapeDtypeStruct((1, query_all), jnp.float32),
+            jax.ShapeDtypeStruct((owners, 1, query_all // owners), jnp.float32),
         ],
+        scratch_shapes=[pltpu.VMEM((1, query_all), jnp.float32)],
         compiler_params=pltpu.CompilerParams(
             dimension_semantics=("arbitrary",), vmem_limit_bytes=60 * 1024 * 1024
         ),
@@ -107,12 +114,10 @@
         counts.reshape(owned, 1),
         all_queries,
         tile,
+        owners,
     )
-    gathered = lax.all_to_all(
-        partial.reshape(owners, query_rows), ("grp", "shard"), split_axis=0, concat_axis=0,
-        tiled=True,
-    )
-    own_best = jnp.min(gathered, axis=0)
+    exchanged = lax.all_to_all(partial, ("grp", "shard"), split_axis=0, concat_axis=0, tiled=True)
+    own_best = jnp.min(exchanged, axis=(0, 1))
     query_norm = jnp.sum(jnp.square(queries.astype(jnp.float32)), axis=1)
     distance = (own_best + query_norm) / features
     return (updated, new_counts.reshape(owned), distance)

time: 136 us -> 133 us (0.978)
    pallas_call x2 -> x1, other arithmetic: 3.51 us -> 2.17 us  [fused_update(): pl.pallas_call(functools.partial(fused_kernel, tile=tile), grid=(steps,),...]
  transfers between devices with their start and end apart: 3 -> 3, of which waited for: 3 -> 3; matrix products, arithmetic and copies ran while one was open for 8% -> 9% of each run, Pallas kernels for 0% -> 0%
where the time goes in v5:
time: 133 us
  waiting for transfers between devices  76.1 us (57%)
  Pallas kernels  17.4 us (13%)
  between operations  14.2 us (11%)
  starting transfers between devices  11.5 us (9%)
  local copies, waits for them, and re-layouts  8.97 us (7%)
  other arithmetic  4.6 us (3%)
    all_gather x1, waiting for transfers between devices, body(): gathered = lax.all_gather(payload, ('grp', 'shard'), axis=0)  68.4 us
    pallas_call x1, Pallas kernels, fused_update(): pl.pallas_call(functools.partial(fused_kernel, tile=tile), grid=(steps,),...  17.4 us
    all_to_all x1, starting transfers between devices, body(): lax.all_to_all(points, ('grp', 'shard'), split_axis=0, concat_axis=0, til...  7.33 us
    all_to_all x1, waiting for transfers between devices, body(): lax.all_to_all(partial, ('grp', 'shard'), split_axis=0, concat_axis=0, ti...  4.89 us
    all_to_all x1, starting transfers between devices, body(): lax.all_to_all(partial, ('grp', 'shard'), split_axis=0, concat_axis=0, ti...  4.17 us
    all_to_all x1, waiting for transfers between devices, body(): lax.all_to_all(points, ('grp', 'shard'), split_axis=0, concat_axis=0, til...  2.78 us
    slice x1, local copies, waits for them, and re-layouts, body(): gathered[:, :query_rows].reshape(owners * query_rows, features)  2.66 us
  transfers between devices with their start and end apart: 3, of which 3 were waited for; matrix products, arithmetic and copies ran while one was open for 9% of the time, Pallas kernels for 0%

profile of v5, /device:TPU:0, one launch (start us, length us, event | category | flops | bytes accessed | tf_op | source)
XLA Modules:
  0.0 132.8 jit_solution(9867612223848821323)
XLA Ops:
  7.2 7.3 %all-to-all-start = ((bf16[32,64,768]{2,1,0:T(8,128)(2,1)}), bf16[32,64,768]{2,1,0:T(8,128)(2,1)S(1)}, u32[]{:S(2)}, u32[]{:S(2)}) async-start(bf16[32,64,768]{2,1,0:T(8,128)(2,1)} %bitcast.10), calls=%async_computation | async-start | bytes 6291456 | tf_op jit(solution)/shard_map/all_to_all | solution.py:96
  14.5 0.0 all-gather.4.cloned.1.call-start
  14.6 0.1 iota_compare_fusion.1
  14.7 0.1 lt.27
  14.8 0.6 maximum_bitcast_fusion
  15.5 0.0 all-gather.4.cloned.1.call-update
  15.5 1.4 %copy.10.counts_ref = f32[2048,1]{1,0:T(8,128)} copy(f32[2048,1]{0,1:T(1,128)S(1)} %bitcast.16) | data formatting | bytes 16384 | tf_op jit(solution)/shard_map/reshape | solution.py:114
  16.9 68.4 %all-gather.4.cloned.1.call-done = bf16[32,38,768]{2,1,0:T(8,128)(2,1)} async-done(((bf16[1,38,768]{2,1,0:T(8,128)(2,1)}), bf16[32,38,768]{2,1,0:T(8,128)(2,1)}) %all-gather.4.cloned.1.call-update) | async-done | bytes 1867792 | tf_op jit(solution)/shard_map/all_gather | solution.py:102
  85.4 1.0 slice.20
  86.4 0.1 copy.11
  86.5 1.3 %reshape.66 = bf16[32,2,32,64]{3,2,1,0:T(8,128)(2,1)} reshape(bf16[32,4096]{1,0:T(8,128)(2,1)S(1)} %slice.21) | data formatting | bytes 524288 | tf_op jit(solution)/shard_map/reshape | solution.py:105
  87.8 0.9 dynamic-slice_convert_fusion
  88.8 0.1 fusion.3
  88.8 0.7 sub.14.ids_ref
  89.5 2.7 %slice.24 = bf16[32,32,768]{2,1,0:T(8,128)(2,1)} slice(bf16[32,38,768]{2,1,0:T(8,128)(2,1)} %all-gather.4.cloned.1.call-done), slice={[0:32], [0:32], [0:768]} | slice | bytes 3145728 | tf_op jit(solution)/shard_map/slice | solution.py:103
  92.2 2.8 %all-to-all-done = bf16[32,64,768]{2,1,0:T(8,128)(2,1)S(1)} async-done(((bf16[32,64,768]{2,1,0:T(8,128)(2,1)}), bf16[32,64,768]{2,1,0:T(8,128)(2,1)S(1)}, u32[]{:S(2)}, u32[]{:S(2)}) %all-to-all-start) | async-done | bytes 3145760 | tf_op jit(solution)/shard_map/all_to_all | solution.py:96
  95.0 1.6 %copy-done = bf16[32,64,768]{2,1,0:T(8,128)(2,1)} copy-done((bf16[32,64,768]{2,1,0:T(8,128)(2,1)}, bf16[32,64,768]{2,1,0:T(8,128)(2,1)S(1)}, u32[]{:S(2)}) %copy-start) | copy-done | bytes 3145752
  96.6 17.4 %shard_map.85 = (f32[2048,768]{1,0:T(8,128)}, f32[2048,1]{1,0:T(8,128)}, f32[32,1,32]{2,1,0:T(1,128)}) custom-call(s32[1,2048]{1,0:T(1,128)} %sub.14.ids_ref, bf16[2048,768]{1,0:T(8,128)(2,1)} %bitcast.11, f32[2048,768]{1,0:T(8,128)} %cent_ref.1, f32[2048,1]{1,0:T(8,128)} %copy.10.counts_ref, bf16[1024,768]{1,0:T(8,128)(2,1)} %bitcast.12), custom_call_target="tpu_custom_call" | custom-call | flops 9663676416 | bytes 17301504 | tf_op jit(solution)/shard_map/pallas_call | solution.py:55
  114.0 4.2 %all-to-all-start.1 = ((f32[32,1,32]{2,1,0:T(1,128)}), f32[32,1,32]{2,1,0:T(1,128)S(1)}, u32[]{:S(2)}, u32[]{:S(2)}) async-start(f32[32,1,32]{2,1,0:T(1,128)} %get-tuple-element.8), calls=%async_computation.1 | async-start | bytes 32768 | tf_op jit(solution)/shard_map/all_to_all | solution.py:119
  118.2 0.1 multiply_reduce_fusion
  118.3 2.2 %reduce.1 = f32[2048]{0:T(1024)} reduce(f32[2048,1]{1,0:T(8,128)} %get-tuple-element.7, f32[]{:T(128)} %constant.62), dimensions={1}, to_apply=%get-tuple-element.7.reduce_sub_computation | reduce | bytes 16388 | tf_op jit(solution)/shard_map/pallas_call | solution.py:55
  120.5 4.9 %all-to-all-done.1 = f32[32,1,32]{2,1,0:T(1,128)S(1)} async-done(((f32[32,1,32]{2,1,0:T(1,128)}), f32[32,1,32]{2,1,0:T(1,128)S(1)}, u32[]{:S(2)}, u32[]{:S(2)}) %all-to-all-start.1) | async-done | bytes 4128 | tf_op jit(solution)/shard_map/all_to_all | solution.py:119
  125.4 0.1 reduce_min.9
  125.4 0.5 add_multiply_fusion
  (13 shorter events, 0.1 us)
Async XLA Ops:
  7.2 7.4 %copy-start.4 = (s32[1,32]{1,0:T(1,128)S(1)}, s32[1,32]{1,0:T(1,128)}, u32[]{:S(2)}) copy-start(s32[1,32]{1,0:T(1,128)} %param.8) | copy-start | bytes 388
  7.2 7.6 %copy-start.3 = (s32[2048]{0:T(1024)S(1)}, s32[2048]{0:T(1024)}, u32[]{:S(2)}) copy-start(s32[2048]{0:T(1024)} %param.7) | copy-start | bytes 24580
  7.2 7.7 %copy-start.1 = (bf16[32,768]{1,0:T(8,128)(2,1)S(1)}, bf16[32,768]{1,0:T(8,128)(2,1)}, u32[]{:S(2)}) copy-start(bf16[32,768]{1,0:T(8,128)(2,1)} %param.11) | copy-start | bytes 147460
  7.2 8.3 %copy-start.2 = (f32[2048]{0:T(1024)S(1)}, f32[2048]{0:T(1024)}, u32[]{:S(2)}) copy-start(f32[2048]{0:T(1024)} %param.10) | copy-start | bytes 24580
  7.2 87.7 %all-to-all-start = ((bf16[32,64,768]{2,1,0:T(8,128)(2,1)}), bf16[32,64,768]{2,1,0:T(8,128)(2,1)S(1)}, u32[]{:S(2)}, u32[]{:S(2)}) async-start(bf16[32,64,768]{2,1,0:T(8,128)(2,1)} %bitcast.10), calls=%async_computation | async-start | bytes 6291456 | tf_op jit(solution)/shard_map/all_to_all | solution.py:96
  14.5 70.8 %all-gather.4.cloned.1.call-start = ((), (), s32[]{:S(2)}) async-start(), calls=%async_computation.2 | async-start | bytes 2027520 | tf_op jit(solution)/shard_map/all_gather | solution.py:102
  95.0 1.7 %copy-start = (bf16[32,64,768]{2,1,0:T(8,128)(2,1)}, bf16[32,64,768]{2,1,0:T(8,128)(2,1)S(1)}, u32[]{:S(2)}) copy-start(bf16[32,64,768]{2,1,0:T(8,128)(2,1)S(1)} %all-to-all-done) | copy-start | bytes 9437188
  114.0 11.4 %all-to-all-start.1 = ((f32[32,1,32]{2,1,0:T(1,128)}), f32[32,1,32]{2,1,0:T(1,128)S(1)}, u32[]{:S(2)}, u32[]{:S(2)}) async-start(f32[32,1,32]{2,1,0:T(1,128)} %get-tuple-element.8), calls=%async_computation.1 | async-start | bytes 32768 | tf_op jit(solution)/shard_map/all_to_all | solution.py:119
Sparse Core Ops, SparseCore 0:
  18.8 66.4 all-gather.3

commit v6 on v5

--- a/solution.py
+++ b/solution.py
@@ -57,7 +57,7 @@
         grid=(steps,),
         in_specs=[
             pl.BlockSpec((1, slots), lambda i: (0, 0)),
-            pl.BlockSpec((slots, features), lambda i: (0, 0)),
+            pl.BlockSpec(memory_space=pltpu.VMEM),
             pl.BlockSpec((tile, features), lambda i: (i, 0)),
             pl.BlockSpec((tile, 1), lambda i: (i, 0)),
             pl.BlockSpec((query_all, features), lambda i: (0, 0)),
@@ -109,7 +109,7 @@
     tile = 512 if owned % 512 == 0 else owned
     updated, new_counts, partial = fused_update(
         arrived_ids.reshape(1, slot_rows),
-        arrived,
+        pltpu.with_memory_space_constraint(arrived, pltpu.VMEM),
         centroids,
         counts.reshape(owned, 1),
         all_queries,

time: 133 us -> 131 us (0.985)
  local copies, waits for them, and re-layouts: 8.97 us -> 7.24 us
    unnamed x11 -> x9, local copies, waits for them, and re-layouts: 1.72 us -> 0.07 us
where the time goes in v6:
time: 131 us; the launch traced here: 130 us
  waiting for transfers between devices  76.2 us (58%)
  Pallas kernels  16.4 us (13%)
  between operations  14.2 us (11%)
  starting transfers between devices  11.5 us (9%)
  local copies, waits for them, and re-layouts  7.24 us (6%)
  other arithmetic  4.6 us (4%)
    all_gather x1, waiting for transfers between devices, body(): gathered = lax.all_gather(payload, ('grp', 'shard'), axis=0)  68.5 us
    pallas_call x1, Pallas kernels, fused_update(): pl.pallas_call(functools.partial(fused_kernel, tile=tile), grid=(steps,),...  16.4 us
    all_to_all x1, starting transfers between devices, body(): lax.all_to_all(points, ('grp', 'shard'), split_axis=0, concat_axis=0, til...  7.33 us
    all_to_all x1, waiting for transfers between devices, body(): lax.all_to_all(partial, ('grp', 'shard'), split_axis=0, concat_axis=0, ti...  4.89 us
    all_to_all x1, starting transfers between devices, body(): lax.all_to_all(partial, ('grp', 'shard'), split_axis=0, concat_axis=0, ti...  4.17 us
    all_to_all x1, waiting for transfers between devices, body(): lax.all_to_all(points, ('grp', 'shard'), split_axis=0, concat_axis=0, til...  2.79 us
    slice x1, local copies, waits for them, and re-layouts, body(): gathered[:, :query_rows].reshape(owners * query_rows, features)  2.66 us
  transfers between devices with their start and end apart: 3, of which 3 were waited for; matrix products, arithmetic and copies ran while one was open for 9% of the time, Pallas kernels for 0%

profile of v6, /device:TPU:0, one launch (start us, length us, event | category | flops | bytes accessed | tf_op | source)
XLA Modules:
  0.0 130.2 jit_solution(17246134984924867918)
XLA Ops:
  7.2 0.0 copy-start.3
  7.2 7.3 %all-to-all-start = ((bf16[32,64,768]{2,1,0:T(8,128)(2,1)}), bf16[32,64,768]{2,1,0:T(8,128)(2,1)S(1)}, u32[]{:S(2)}, u32[]{:S(2)}) async-start(bf16[32,64,768]{2,1,0:T(8,128)(2,1)} %bitcast.11), calls=%async_computation | async-start | bytes 6291456 | tf_op jit(solution)/shard_map/all_to_all | solution.py:96
  14.5 0.0 all-gather.4.cloned.1.call-start
  14.6 0.1 iota_compare_fusion.1
  14.7 0.1 lt.27
  14.8 0.6 maximum_bitcast_fusion
  15.5 0.0 all-gather.4.cloned.1.call-update
  15.5 1.3 %copy.10.counts_ref = f32[2048,1]{1,0:T(8,128)} copy(f32[2048,1]{0,1:T(1,128)S(1)} %bitcast.16) | data formatting | bytes 16384 | tf_op jit(solution)/shard_map/reshape | solution.py:114
  16.9 68.5 %all-gather.4.cloned.1.call-done = bf16[32,38,768]{2,1,0:T(8,128)(2,1)} async-done(((bf16[1,38,768]{2,1,0:T(8,128)(2,1)}), bf16[32,38,768]{2,1,0:T(8,128)(2,1)}) %all-gather.4.cloned.1.call-update) | async-done | bytes 1867792 | tf_op jit(solution)/shard_map/all_gather | solution.py:102
  85.4 1.0 slice.20
  86.4 0.1 copy.11
  86.5 1.3 %reshape.66 = bf16[32,2,32,64]{3,2,1,0:T(8,128)(2,1)} reshape(bf16[32,4096]{1,0:T(8,128)(2,1)S(1)} %slice.21) | data formatting | bytes 524288 | tf_op jit(solution)/shard_map/reshape | solution.py:105
  87.8 0.9 dynamic-slice_convert_fusion
  88.8 0.1 fusion.3
  88.8 0.7 sub.14.ids_ref
  89.5 2.7 %slice.24 = bf16[32,32,768]{2,1,0:T(8,128)(2,1)} slice(bf16[32,38,768]{2,1,0:T(8,128)(2,1)} %all-gather.4.cloned.1.call-done), slice={[0:32], [0:32], [0:768]} | slice | bytes 3145728 | tf_op jit(solution)/shard_map/slice | solution.py:103
  92.2 2.8 %all-to-all-done = bf16[32,64,768]{2,1,0:T(8,128)(2,1)S(1)} async-done(((bf16[32,64,768]{2,1,0:T(8,128)(2,1)}), bf16[32,64,768]{2,1,0:T(8,128)(2,1)S(1)}, u32[]{:S(2)}, u32[]{:S(2)}) %all-to-all-start) | async-done | bytes 3145760 | tf_op jit(solution)/shard_map/all_to_all | solution.py:96
  95.0 16.4 %shard_map.85 = (f32[2048,768]{1,0:T(8,128)}, f32[2048,1]{1,0:T(8,128)}, f32[32,1,32]{2,1,0:T(1,128)}) custom-call(s32[1,2048]{1,0:T(1,128)} %sub.14.ids_ref, bf16[2048,768]{1,0:T(8,128)(2,1)S(1)} %bitcast.10, f32[2048,768]{1,0:T(8,128)} %cent_ref.1, f32[2048,1]{1,0:T(8,128)} %copy.10.counts_ref, bf16[1024,768]{1,0:T(8,128)(2,1)} %bitcast.12), custom_call_target="tpu_custom_call" | custom-call | flops 9663676416 | bytes 17301504 | tf_op jit(solution)/shard_map/pallas_call | solution.py:55
  111.4 4.2 %all-to-all-start.1 = ((f32[32,1,32]{2,1,0:T(1,128)}), f32[32,1,32]{2,1,0:T(1,128)S(1)}, u32[]{:S(2)}, u32[]{:S(2)}) async-start(f32[32,1,32]{2,1,0:T(1,128)} %get-tuple-element.8), calls=%async_computation.1 | async-start | bytes 32768 | tf_op jit(solution)/shard_map/all_to_all | solution.py:119
  115.6 0.1 multiply_reduce_fusion
  115.7 2.2 %reduce.1 = f32[2048]{0:T(1024)} reduce(f32[2048,1]{1,0:T(8,128)} %get-tuple-element.7, f32[]{:T(128)} %constant.62), dimensions={1}, to_apply=%get-tuple-element.7.reduce_sub_computation | reduce | bytes 16388 | tf_op jit(solution)/shard_map/pallas_call | solution.py:55
  117.9 4.9 %all-to-all-done.1 = f32[32,1,32]{2,1,0:T(1,128)S(1)} async-done(((f32[32,1,32]{2,1,0:T(1,128)}), f32[32,1,32]{2,1,0:T(1,128)S(1)}, u32[]{:S(2)}, u32[]{:S(2)}) %all-to-all-start.1) | async-done | bytes 4128 | tf_op jit(solution)/shard_map/all_to_all | solution.py:119
  122.8 0.1 reduce_min.9
  122.8 0.5 add_multiply_fusion
  (11 shorter events, 0.1 us)
Async XLA Ops:
  7.2 7.4 %copy-start.3 = (s32[1,32]{1,0:T(1,128)S(1)}, s32[1,32]{1,0:T(1,128)}, u32[]{:S(2)}) copy-start(s32[1,32]{1,0:T(1,128)} %param.8) | copy-start | bytes 388
  7.2 7.6 %copy-start.2 = (s32[2048]{0:T(1024)S(1)}, s32[2048]{0:T(1024)}, u32[]{:S(2)}) copy-start(s32[2048]{0:T(1024)} %param.7) | copy-start | bytes 24580
  7.2 7.7 %copy-start = (bf16[32,768]{1,0:T(8,128)(2,1)S(1)}, bf16[32,768]{1,0:T(8,128)(2,1)}, u32[]{:S(2)}) copy-start(bf16[32,768]{1,0:T(8,128)(2,1)} %param.11) | copy-start | bytes 147460
  7.2 8.3 %copy-start.1 = (f32[2048]{0:T(1024)S(1)}, f32[2048]{0:T(1024)}, u32[]{:S(2)}) copy-start(f32[2048]{0:T(1024)} %param.10) | copy-start | bytes 24580
  7.2 87.7 %all-to-all-start = ((bf16[32,64,768]{2,1,0:T(8,128)(2,1)}), bf16[32,64,768]{2,1,0:T(8,128)(2,1)S(1)}, u32[]{:S(2)}, u32[]{:S(2)}) async-start(bf16[32,64,768]{2,1,0:T(8,128)(2,1)} %bitcast.11), calls=%async_computation | async-start | bytes 6291456 | tf_op jit(solution)/shard_map/all_to_all | solution.py:96
  14.5 70.8 %all-gather.4.cloned.1.call-start = ((), (), s32[]{:S(2)}) async-start(), calls=%async_computation.2 | async-start | bytes 2027520 | tf_op jit(solution)/shard_map/all_gather | solution.py:102
  111.4 11.4 %all-to-all-start.1 = ((f32[32,1,32]{2,1,0:T(1,128)}), f32[32,1,32]{2,1,0:T(1,128)S(1)}, u32[]{:S(2)}, u32[]{:S(2)}) async-start(f32[32,1,32]{2,1,0:T(1,128)} %get-tuple-element.8), calls=%async_computation.1 | async-start | bytes 32768 | tf_op jit(solution)/shard_map/all_to_all | solution.py:119
Sparse Core Ops, SparseCore 0:
  18.8 66.4 all-gather.3

commit v7 on v6

--- a/solution.py
+++ b/solution.py
@@ -19,7 +19,8 @@
     hits = jnp.sum(onehot, axis=1, keepdims=True)
     cent = cent_ref[...]
     new_counts = counts_ref[...] + hits
-    updated = cent + (sums - hits * cent) / new_counts
+    scale = 1.0 / new_counts
+    updated = cent + (sums - hits * cent) * scale
     upd_ref[...] = updated
     nc_ref[...] = new_counts
     rounded = updated.astype(jnp.bfloat16)

time: 131 us -> 131 us (level)
  no operation moved by 1% of the time
where the time goes in v7:
time: 131 us; the launch traced here: 130 us
  waiting for transfers between devices  76.2 us (58%)
  Pallas kernels  16.4 us (13%)
  between operations  14.2 us (11%)
  starting transfers between devices  11.5 us (9%)
  local copies, waits for them, and re-layouts  7.24 us (6%)
  other arithmetic  4.6 us (4%)
    all_gather x1, waiting for transfers between devices, body(): gathered = lax.all_gather(payload, ('grp', 'shard'), axis=0)  68.5 us
    pallas_call x1, Pallas kernels, fused_update(): pl.pallas_call(functools.partial(fused_kernel, tile=tile), grid=(steps,),...  16.4 us
    all_to_all x1, starting transfers between devices, body(): lax.all_to_all(points, ('grp', 'shard'), split_axis=0, concat_axis=0, til...  7.33 us
    all_to_all x1, waiting for transfers between devices, body(): lax.all_to_all(partial, ('grp', 'shard'), split_axis=0, concat_axis=0, ti...  4.89 us
    all_to_all x1, starting transfers between devices, body(): lax.all_to_all(partial, ('grp', 'shard'), split_axis=0, concat_axis=0, ti...  4.17 us
    all_to_all x1, waiting for transfers between devices, body(): lax.all_to_all(points, ('grp', 'shard'), split_axis=0, concat_axis=0, til...  2.79 us
    slice x1, local copies, waits for them, and re-layouts, body(): gathered[:, :query_rows].reshape(owners * query_rows, features)  2.66 us
  transfers between devices with their start and end apart: 3, of which 3 were waited for; matrix products, arithmetic and copies ran while one was open for 9% of the time, Pallas kernels for 0%

profile of v7, /device:TPU:0, one launch (start us, length us, event | category | flops | bytes accessed | tf_op | source)
XLA Modules:
  0.0 130.2 jit_solution(7238847664355246987)
XLA Ops:
  7.2 0.0 copy-start.3
  7.2 7.3 %all-to-all-start = ((bf16[32,64,768]{2,1,0:T(8,128)(2,1)}), bf16[32,64,768]{2,1,0:T(8,128)(2,1)S(1)}, u32[]{:S(2)}, u32[]{:S(2)}) async-start(bf16[32,64,768]{2,1,0:T(8,128)(2,1)} %bitcast.11), calls=%async_computation | async-start | bytes 6291456 | tf_op jit(solution)/shard_map/all_to_all | solution.py:97
  14.5 0.0 all-gather.4.cloned.1.call-start
  14.6 0.1 iota_compare_fusion.1
  14.7 0.1 lt.27
  14.8 0.6 maximum_bitcast_fusion
  15.5 0.0 all-gather.4.cloned.1.call-update
  15.5 1.3 %copy.10.counts_ref = f32[2048,1]{1,0:T(8,128)} copy(f32[2048,1]{0,1:T(1,128)S(1)} %bitcast.16) | data formatting | bytes 16384 | tf_op jit(solution)/shard_map/reshape | solution.py:115
  16.9 68.5 %all-gather.4.cloned.1.call-done = bf16[32,38,768]{2,1,0:T(8,128)(2,1)} async-done(((bf16[1,38,768]{2,1,0:T(8,128)(2,1)}), bf16[32,38,768]{2,1,0:T(8,128)(2,1)}) %all-gather.4.cloned.1.call-update) | async-done | bytes 1867792 | tf_op jit(solution)/shard_map/all_gather | solution.py:103
  85.4 1.0 slice.20
  86.4 0.1 copy.11
  86.5 1.3 %reshape.66 = bf16[32,2,32,64]{3,2,1,0:T(8,128)(2,1)} reshape(bf16[32,4096]{1,0:T(8,128)(2,1)S(1)} %slice.21) | data formatting | bytes 524288 | tf_op jit(solution)/shard_map/reshape | solution.py:106
  87.8 0.9 dynamic-slice_convert_fusion
  88.8 0.1 fusion.3
  88.8 0.7 sub.14.ids_ref
  89.5 2.7 %slice.24 = bf16[32,32,768]{2,1,0:T(8,128)(2,1)} slice(bf16[32,38,768]{2,1,0:T(8,128)(2,1)} %all-gather.4.cloned.1.call-done), slice={[0:32], [0:32], [0:768]} | slice | bytes 3145728 | tf_op jit(solution)/shard_map/slice | solution.py:104
  92.2 2.8 %all-to-all-done = bf16[32,64,768]{2,1,0:T(8,128)(2,1)S(1)} async-done(((bf16[32,64,768]{2,1,0:T(8,128)(2,1)}), bf16[32,64,768]{2,1,0:T(8,128)(2,1)S(1)}, u32[]{:S(2)}, u32[]{:S(2)}) %all-to-all-start) | async-done | bytes 3145760 | tf_op jit(solution)/shard_map/all_to_all | solution.py:97
  95.0 16.4 %shard_map.85 = (f32[2048,768]{1,0:T(8,128)}, f32[2048,1]{1,0:T(8,128)}, f32[32,1,32]{2,1,0:T(1,128)}) custom-call(s32[1,2048]{1,0:T(1,128)} %sub.14.ids_ref, bf16[2048,768]{1,0:T(8,128)(2,1)S(1)} %bitcast.10, f32[2048,768]{1,0:T(8,128)} %cent_ref.1, f32[2048,1]{1,0:T(8,128)} %copy.10.counts_ref, bf16[1024,768]{1,0:T(8,128)(2,1)} %bitcast.12), custom_call_target="tpu_custom_call" | custom-call | flops 9663676416 | bytes 17301504 | tf_op jit(solution)/shard_map/pallas_call | solution.py:56
  111.4 4.2 %all-to-all-start.1 = ((f32[32,1,32]{2,1,0:T(1,128)}), f32[32,1,32]{2,1,0:T(1,128)S(1)}, u32[]{:S(2)}, u32[]{:S(2)}) async-start(f32[32,1,32]{2,1,0:T(1,128)} %get-tuple-element.8), calls=%async_computation.1 | async-start | bytes 32768 | tf_op jit(solution)/shard_map/all_to_all | solution.py:120
  115.6 0.1 multiply_reduce_fusion
  115.7 2.2 %reduce.1 = f32[2048]{0:T(1024)} reduce(f32[2048,1]{1,0:T(8,128)} %get-tuple-element.7, f32[]{:T(128)} %constant.62), dimensions={1}, to_apply=%get-tuple-element.7.reduce_sub_computation | reduce | bytes 16388 | tf_op jit(solution)/shard_map/pallas_call | solution.py:56
  117.9 4.9 %all-to-all-done.1 = f32[32,1,32]{2,1,0:T(1,128)S(1)} async-done(((f32[32,1,32]{2,1,0:T(1,128)}), f32[32,1,32]{2,1,0:T(1,128)S(1)}, u32[]{:S(2)}, u32[]{:S(2)}) %all-to-all-start.1) | async-done | bytes 4128 | tf_op jit(solution)/shard_map/all_to_all | solution.py:120
  122.7 0.1 reduce_min.9
  122.8 0.5 add_multiply_fusion
  (11 shorter events, 0.1 us)
Async XLA Ops:
  7.2 7.4 %copy-start.3 = (s32[1,32]{1,0:T(1,128)S(1)}, s32[1,32]{1,0:T(1,128)}, u32[]{:S(2)}) copy-start(s32[1,32]{1,0:T(1,128)} %param.8) | copy-start | bytes 388
  7.2 7.6 %copy-start.2 = (s32[2048]{0:T(1024)S(1)}, s32[2048]{0:T(1024)}, u32[]{:S(2)}) copy-start(s32[2048]{0:T(1024)} %param.7) | copy-start | bytes 24580
  7.2 7.7 %copy-start = (bf16[32,768]{1,0:T(8,128)(2,1)S(1)}, bf16[32,768]{1,0:T(8,128)(2,1)}, u32[]{:S(2)}) copy-start(bf16[32,768]{1,0:T(8,128)(2,1)} %param.11) | copy-start | bytes 147460
  7.2 8.3 %copy-start.1 = (f32[2048]{0:T(1024)S(1)}, f32[2048]{0:T(1024)}, u32[]{:S(2)}) copy-start(f32[2048]{0:T(1024)} %param.10) | copy-start | bytes 24580
  7.2 87.7 %all-to-all-start = ((bf16[32,64,768]{2,1,0:T(8,128)(2,1)}), bf16[32,64,768]{2,1,0:T(8,128)(2,1)S(1)}, u32[]{:S(2)}, u32[]{:S(2)}) async-start(bf16[32,64,768]{2,1,0:T(8,128)(2,1)} %bitcast.11), calls=%async_computation | async-start | bytes 6291456 | tf_op jit(solution)/shard_map/all_to_all | solution.py:97
  14.5 70.8 %all-gather.4.cloned.1.call-start = ((), (), s32[]{:S(2)}) async-start(), calls=%async_computation.2 | async-start | bytes 2027520 | tf_op jit(solution)/shard_map/all_gather | solution.py:103
  111.4 11.4 %all-to-all-start.1 = ((f32[32,1,32]{2,1,0:T(1,128)}), f32[32,1,32]{2,1,0:T(1,128)S(1)}, u32[]{:S(2)}, u32[]{:S(2)}) async-start(f32[32,1,32]{2,1,0:T(1,128)} %get-tuple-element.8), calls=%async_computation.1 | async-start | bytes 32768 | tf_op jit(solution)/shard_map/all_to_all | solution.py:120
Sparse Core Ops, SparseCore 0:
  18.8 66.4 all-gather.3

commit v8 on v6

--- a/solution.py
+++ b/solution.py
@@ -95,17 +95,21 @@
     )
     arrived = lax.all_to_all(points, ("grp", "shard"), split_axis=0, concat_axis=0, tiled=True)
     shifted = tagged + 1
-    codes = jnp.concatenate([shifted // 64, shifted % 64]).astype(jnp.bfloat16)
+    level, offset = shifted // 128, shifted % 128
+    up = jnp.asarray([2.0 ** (k - 7) for k in range(17)], jnp.float32)
+    codes = ((offset + 128).astype(jnp.float32) * up[level]).astype(jnp.bfloat16)
     code_rows = -(-codes.shape[0] // features)
     codes = jnp.pad(codes, (0, code_rows * features - codes.shape[0]))
     payload = jnp.concatenate([queries, codes.reshape(code_rows, features)], axis=0)
     gathered = lax.all_gather(payload, ("grp", "shard"), axis=0)
     all_queries = gathered[:, :query_rows].reshape(owners * query_rows, features)
-    received = gathered[:, query_rows:].reshape(owners, code_rows * features)[:, : 2 * slot_rows]
-    received = received.reshape(owners, 2, owners, capacity)
-    mine = lax.dynamic_index_in_dim(received, lax.axis_index(("grp", "shard")), 2, keepdims=False)
-    mine = mine.astype(jnp.int32)
-    arrived_ids = mine[:, 0] * 64 + mine[:, 1] - 1
+    received = gathered[:, query_rows:].reshape(owners, code_rows * features)[:, :slot_rows]
+    received = received.reshape(owners, owners, capacity)
+    mine = lax.dynamic_index_in_dim(received, lax.axis_index(("grp", "shard")), 1, keepdims=False)
+    mine = mine.astype(jnp.float32)
+    found = sum((mine >= 2.0**k).astype(jnp.int32) for k in range(1, 17))
+    down = jnp.asarray([2.0 ** (7 - k) for k in range(17)], jnp.float32)
+    arrived_ids = found * 128 + (mine * down[found]).astype(jnp.int32) - 128 - 1
     tile = 512 if owned % 512 == 0 else owned
     updated, new_counts, partial = fused_update(
         arrived_ids.reshape(1, slot_rows),

time: 131 us -> 139 us (1.061)
  local copies, waits for them, and re-layouts: 7.24 us -> 18.2 us
  waiting for transfers between devices: 76.2 us -> 73.4 us
    gather x0 -> x1, local copies, waits for them, and re-layouts: none -> 12.6 us  [body(): arrived_ids = found * 128 + (mine * down[found]).astype(jnp.int32) - 128 - 1]
    all_to_all x1, waiting for transfers between devices: 2.79 us -> 0.01 us  [body(): lax.all_to_all(points, ('grp', 'shard'), split_axis=0, concat_axis=0, til...]
  transfers between devices with their start and end apart: 3 -> 3, of which waited for: 3 -> 2; matrix products, arithmetic and copies ran while one was open for 9% -> 16% of each run, Pallas kernels for 0% -> 0%
where the time goes in v8:
time: 139 us
  waiting for transfers between devices  73.4 us (53%)
  local copies, waits for them, and re-layouts  18.2 us (13%)
  Pallas kernels  16.5 us (12%)
  between operations  14.2 us (10%)
  starting transfers between devices  12.4 us (9%)
  other arithmetic  4.36 us (3%)
    all_gather x1, waiting for transfers between devices, body(): gathered = lax.all_gather(payload, ('grp', 'shard'), axis=0)  68.5 us
    pallas_call x1, Pallas kernels, fused_update(): pl.pallas_call(functools.partial(fused_kernel, tile=tile), grid=(steps,),...  16.5 us
    gather x1, local copies, waits for them, and re-layouts, body(): arrived_ids = found * 128 + (mine * down[found]).astype(jnp.int32) - 128 - 1  12.6 us
    all_to_all x1, starting transfers between devices, body(): lax.all_to_all(points, ('grp', 'shard'), split_axis=0, concat_axis=0, til...  7.33 us
    all_to_all x1, starting transfers between devices, body(): lax.all_to_all(partial, ('grp', 'shard'), split_axis=0, concat_axis=0, ti...  5.07 us
    all_to_all x1, waiting for transfers between devices, body(): lax.all_to_all(partial, ('grp', 'shard'), split_axis=0, concat_axis=0, ti...  4.87 us
  transfers between devices with their start and end apart: 3, of which 2 were waited for; matrix products, arithmetic and copies ran while one was open for 16% of the time, Pallas kernels for 0%

profile of v8, /device:TPU:0, one launch (start us, length us, event | category | flops | bytes accessed | tf_op | source)
XLA Modules:
  0.0 139.1 jit_solution(17937332979645559480)
XLA Ops:
  7.2 0.0 copy-start.1
  7.2 0.0 copy-start
  7.2 7.3 %all-to-all-start = ((bf16[32,64,768]{2,1,0:T(8,128)(2,1)}), bf16[32,64,768]{2,1,0:T(8,128)(2,1)S(1)}, u32[]{:S(2)}, u32[]{:S(2)}) async-start(bf16[32,64,768]{2,1,0:T(8,128)(2,1)} %bitcast.29), calls=%async_computation | async-start | bytes 6291456 | tf_op jit(solution)/shard_map/all_to_all | solution.py:96
  14.6 0.0 all-gather.4.cloned.1.call-start
  14.6 0.1 iota_compare_fusion
  14.7 0.1 lt.44
  14.9 0.6 maximum_bitcast_fusion
  15.5 0.0 all-gather.4.cloned.1.call-update
  15.5 1.3 copy.44.counts_ref
  16.9 68.5 %all-gather.4.cloned.1.call-done = bf16[32,35,768]{2,1,0:T(8,128)(2,1)} async-done(((bf16[1,35,768]{2,1,0:T(8,128)(2,1)}), bf16[32,35,768]{2,1,0:T(8,128)(2,1)}) %all-gather.4.cloned.1.call-update) | async-done | bytes 1720336 | tf_op jit(solution)/shard_map/all_gather | solution.py:104
  85.4 1.0 slice.32
  86.5 0.2 reshape.435
  86.8 0.1 reshape.483
  86.9 0.1 reshape.439
  87.0 12.6 %gather_fusion = f32[2048]{0:T(1024)S(1)} fusion(f32[17]{0:T(128)S(1)} %copy-done, s32[2048]{0:T(1024)S(1)} %broadcast_clamp_fusion), kind=kCustom, calls=%fused_computation | custom fusion | bytes 24576 | tf_op jit(solution)/shard_map/gather | solution.py:112
  99.6 2.7 %slice.34 = bf16[32,32,768]{2,1,0:T(8,128)(2,1)} slice(bf16[32,35,768]{2,1,0:T(8,128)(2,1)} %all-gather.4.cloned.1.call-done), slice={[0:32], [0:32], [0:768]} | slice | bytes 3145728 | tf_op jit(solution)/shard_map/slice | solution.py:105
  102.3 0.7 fusion.21.ids_ref
  103.0 16.5 %shard_map.103 = (f32[2048,768]{1,0:T(8,128)}, f32[2048,1]{1,0:T(8,128)}, f32[32,1,32]{2,1,0:T(1,128)}) custom-call(s32[1,2048]{1,0:T(1,128)} %fusion.21.ids_ref, bf16[2048,768]{1,0:T(8,128)(2,1)S(1)} %bitcast.28, f32[2048,768]{1,0:T(8,128)} %cent_ref.1, f32[2048,1]{1,0:T(8,128)} %copy.44.counts_ref, bf16[1024,768]{1,0:T(8,128)(2,1)} %bitcast.30), custom_call_target="tpu_custom_call" | custom-call | flops 9663676416 | bytes 17301504 | tf_op jit(solution)/shard_map/pallas_call | solution.py:55
  119.5 5.1 %all-to-all-start.1 = ((f32[32,1,32]{2,1,0:T(1,128)}), f32[32,1,32]{2,1,0:T(1,128)S(1)}, u32[]{:S(2)}, u32[]{:S(2)}) async-start(f32[32,1,32]{2,1,0:T(1,128)} %get-tuple-element.8), calls=%async_computation.1 | async-start | bytes 32768 | tf_op jit(solution)/shard_map/all_to_all | solution.py:123
  124.5 0.1 multiply_reduce_fusion
  124.7 2.2 %reduce = f32[2048]{0:T(1024)} reduce(f32[2048,1]{1,0:T(8,128)} %get-tuple-element.7, f32[]{:T(128)} %constant.161), dimensions={1}, to_apply=%get-tuple-element.7.reduce_sub_computation | reduce | bytes 16388 | tf_op jit(solution)/shard_map/pallas_call | solution.py:55
  126.8 4.9 %all-to-all-done.1 = f32[32,1,32]{2,1,0:T(1,128)S(1)} async-done(((f32[32,1,32]{2,1,0:T(1,128)}), f32[32,1,32]{2,1,0:T(1,128)S(1)}, u32[]{:S(2)}, u32[]{:S(2)}) %all-to-all-start.1) | async-done | bytes 4128 | tf_op jit(solution)/shard_map/all_to_all | solution.py:123
  131.7 0.1 reduce_min.9
  131.8 0.5 add_multiply_fusion
  (20 shorter events, 0.2 us)
Async XLA Ops:
  7.2 7.4 %copy-start.5 = (s32[1,32]{1,0:T(1,128)S(1)}, s32[1,32]{1,0:T(1,128)}, u32[]{:S(2)}) copy-start(s32[1,32]{1,0:T(1,128)} %param.10) | copy-start | bytes 388
  7.2 7.6 %copy-start.4 = (s32[2048]{0:T(1024)S(1)}, s32[2048]{0:T(1024)}, u32[]{:S(2)}) copy-start(s32[2048]{0:T(1024)} %param.9) | copy-start | bytes 24580
  7.2 7.7 %copy-start.1 = (bf16[32,768]{1,0:T(8,128)(2,1)S(1)}, bf16[32,768]{1,0:T(8,128)(2,1)}, u32[]{:S(2)}) copy-start(bf16[32,768]{1,0:T(8,128)(2,1)} %param.13) | copy-start | bytes 147460
  7.2 8.3 %copy-start.3 = (f32[2048]{0:T(1024)S(1)}, f32[2048]{0:T(1024)}, u32[]{:S(2)}) copy-start(f32[2048]{0:T(1024)} %param.12) | copy-start | bytes 24580
  7.2 79.8 %copy-start = (f32[17]{0:T(128)S(1)}, f32[17]{0:T(128)}, u32[]{:S(2)}) copy-start(f32[17]{0:T(128)} %constant.104.clone) | copy-start | bytes 208
  7.2 95.8 %all-to-all-start = ((bf16[32,64,768]{2,1,0:T(8,128)(2,1)}), bf16[32,64,768]{2,1,0:T(8,128)(2,1)S(1)}, u32[]{:S(2)}, u32[]{:S(2)}) async-start(bf16[32,64,768]{2,1,0:T(8,128)(2,1)} %bitcast.29), calls=%async_computation | async-start | bytes 6291456 | tf_op jit(solution)/shard_map/all_to_all | solution.py:96
  14.6 70.8 %all-gather.4.cloned.1.call-start = ((), (), s32[]{:S(2)}) async-start(), calls=%async_computation.2 | async-start | bytes 2027520 | tf_op jit(solution)/shard_map/all_gather | solution.py:104
  103.0 21.6 %copy-start.2 = (bf16[32,768]{1,0:T(8,128)(2,1)S(1)}, bf16[32,768]{1,0:T(8,128)(2,1)}, u32[]{:S(2)}) copy-start(bf16[32,768]{1,0:T(8,128)(2,1)} %param.13) | copy-start | bytes 147460
  119.5 12.2 %all-to-all-start.1 = ((f32[32,1,32]{2,1,0:T(1,128)}), f32[32,1,32]{2,1,0:T(1,128)S(1)}, u32[]{:S(2)}, u32[]{:S(2)}) async-start(f32[32,1,32]{2,1,0:T(1,128)} %get-tuple-element.8), calls=%async_computation.1 | async-start | bytes 32768 | tf_op jit(solution)/shard_map/all_to_all | solution.py:123
Sparse Core Ops, SparseCore 0:
  18.8 66.4 all-gather.3

commit v9 on v6

--- a/solution.py
+++ b/solution.py
@@ -26,7 +26,10 @@
     wide = rounded.astype(jnp.float32)
     norm = jnp.sum(wide * wide, axis=1, keepdims=True)
     inner = lax.dot_general(
-        rounded, q_ref[...], (((1,), (1,)), ((), ())), preferred_element_type=jnp.float32
+        rounded,
+        q_ref[...].reshape(-1, q_ref.shape[2]),
+        (((1,), (1,)), ((), ())),
+        preferred_element_type=jnp.float32,
     )
     least = jnp.min(norm - 2.0 * inner, axis=0, keepdims=True)
 
@@ -45,13 +48,14 @@
             min_ref[owner] = run_ref[:, owner * query_rows : (owner + 1) * query_rows]
 
 
-def fused_update(ids_row, rows, centroids, counts_col, all_queries, tile, owners):
+def fused_update(ids_row, rows, centroids, counts_col, gathered, query_rows, tile):
     owned, features = centroids.shape
     slots = rows.shape[0]
-    query_all = all_queries.shape[0]
+    owners = gathered.shape[0]
+    query_all = owners * query_rows
     steps = owned // tile
     flops = 2 * owned * slots * features + 2 * owned * query_all * features
-    moved = rows.size * 2 + centroids.size * 8 + all_queries.size * 2
+    moved = rows.size * 2 + centroids.size * 8 + query_all * features * 2
     return pl.pallas_call(
         functools.partial(fused_kernel, tile=tile),
         grid=(steps,),
@@ -60,7 +64,7 @@
             pl.BlockSpec(memory_space=pltpu.VMEM),
             pl.BlockSpec((tile, features), lambda i: (i, 0)),
             pl.BlockSpec((tile, 1), lambda i: (i, 0)),
-            pl.BlockSpec((query_all, features), lambda i: (0, 0)),
+            pl.BlockSpec((owners, query_rows, features), lambda i: (0, 0, 0)),
         ],
         out_specs=[
             pl.BlockSpec((tile, features), lambda i: (i, 0)),
@@ -77,7 +81,7 @@
             dimension_semantics=("arbitrary",), vmem_limit_bytes=60 * 1024 * 1024
         ),
         cost_estimate=pl.CostEstimate(flops=flops, bytes_accessed=moved, transcendentals=0),
-    )(ids_row, rows, centroids, counts_col, all_queries)
+    )(ids_row, rows, centroids, counts_col, gathered)
 
 
 def body(points, local_ids, block_counts, centroids, counts, queries):
@@ -100,7 +104,6 @@
     codes = jnp.pad(codes, (0, code_rows * features - codes.shape[0]))
     payload = jnp.concatenate([queries, codes.reshape(code_rows, features)], axis=0)
     gathered = lax.all_gather(payload, ("grp", "shard"), axis=0)
-    all_queries = gathered[:, :query_rows].reshape(owners * query_rows, features)
     received = gathered[:, query_rows:].reshape(owners, code_rows * features)[:, : 2 * slot_rows]
     received = received.reshape(owners, 2, owners, capacity)
     mine = lax.dynamic_index_in_dim(received, lax.axis_index(("grp", "shard")), 2, keepdims=False)
@@ -112,9 +115,9 @@
         pltpu.with_memory_space_constraint(arrived, pltpu.VMEM),
         centroids,
         counts.reshape(owned, 1),
-        all_queries,
+        gathered,
+        query_rows,
         tile,
-        owners,
     )
     exchanged = lax.all_to_all(partial, ("grp", "shard"), split_axis=0, concat_axis=0, tiled=True)
     own_best = jnp.min(exchanged, axis=(0, 1))

time: 131 us -> 131 us (level)
  waiting for transfers between devices: 76.2 us -> 78.9 us
  local copies, waits for them, and re-layouts: 7.24 us -> 5.54 us
    all_to_all x1, waiting for transfers between devices: 2.79 us -> 5.49 us  [body(): lax.all_to_all(points, ('grp', 'shard'), split_axis=0, concat_axis=0, til...]
    slice x1 -> x0, local copies, waits for them, and re-layouts: 2.66 us -> none  [body(): gathered[:, :query_rows].reshape(owners * query_rows, features)]
  transfers between devices with their start and end apart: 3 -> 3, of which waited for: 3 -> 3; matrix products, arithmetic and copies ran while one was open for 9% -> 7% of each run, Pallas kernels for 0% -> 0%
where the time goes in v9:
time: 131 us; the launch traced here: 130 us
  waiting for transfers between devices  78.9 us (60%)
  Pallas kernels  16.5 us (13%)
  between operations  14.2 us (11%)
  starting transfers between devices  11.5 us (9%)
  local copies, waits for them, and re-layouts  5.54 us (4%)
  other arithmetic  3.6 us (3%)
    all_gather x1, waiting for transfers between devices, body(): gathered = lax.all_gather(payload, ('grp', 'shard'), axis=0)  68.5 us
    pallas_call x1, Pallas kernels, fused_update(): pl.pallas_call(functools.partial(fused_kernel, tile=tile), grid=(steps,),...  16.5 us
    all_to_all x1, starting transfers between devices, body(): lax.all_to_all(points, ('grp', 'shard'), split_axis=0, concat_axis=0, til...  7.33 us
    all_to_all x1, waiting for transfers between devices, body(): lax.all_to_all(points, ('grp', 'shard'), split_axis=0, concat_axis=0, til...  5.49 us
    all_to_all x1, waiting for transfers between devices, body(): lax.all_to_all(partial, ('grp', 'shard'), split_axis=0, concat_axis=0, ti...  4.88 us
    all_to_all x1, starting transfers between devices, body(): lax.all_to_all(partial, ('grp', 'shard'), split_axis=0, concat_axis=0, ti...  4.17 us
  transfers between devices with their start and end apart: 3, of which 3 were waited for; matrix products, arithmetic and copies ran while one was open for 7% of the time, Pallas kernels for 0%

profile of v9, /device:TPU:0, one launch (start us, length us, event | category | flops | bytes accessed | tf_op | source)
XLA Modules:
  0.0 130.2 jit_solution(2335305429327407323)
XLA Ops:
  7.2 0.0 copy-start.3
  7.2 0.0 copy-start.2
  7.2 0.0 copy-start
  7.2 7.3 %all-to-all-start = ((bf16[32,64,768]{2,1,0:T(8,128)(2,1)}), bf16[32,64,768]{2,1,0:T(8,128)(2,1)S(1)}, u32[]{:S(2)}, u32[]{:S(2)}) async-start(bf16[32,64,768]{2,1,0:T(8,128)(2,1)} %bitcast.16), calls=%async_computation | async-start | bytes 6291456 | tf_op jit(solution)/shard_map/all_to_all | solution.py:100
  14.5 0.0 all-gather.4.cloned.1.call-start
  14.6 0.1 iota_compare_fusion.1
  14.7 0.1 lt.27
  14.8 0.6 maximum_bitcast_fusion
  15.5 0.0 all-gather.4.cloned.1.call-update
  15.5 1.4 %copy.13.counts_ref = f32[2048,1]{1,0:T(8,128)} copy(f32[2048,1]{0,1:T(1,128)S(1)} %bitcast.19) | data formatting | bytes 16384 | tf_op jit(solution)/shard_map/reshape | solution.py:117
  16.9 68.5 %all-gather.4.cloned.1.call-done.q_ref = bf16[32,38,768]{2,1,0:T(8,128)(2,1)} async-done(((bf16[1,38,768]{2,1,0:T(8,128)(2,1)}), bf16[32,38,768]{2,1,0:T(8,128)(2,1)}) %all-gather.4.cloned.1.call-update) | async-done | bytes 1867792 | tf_op jit(solution)/shard_map/all_gather | solution.py:106
  85.4 1.0 slice.16
  86.4 0.1 copy.15
  86.5 1.3 %reshape.63 = bf16[32,2,32,64]{3,2,1,0:T(8,128)(2,1)} reshape(bf16[32,4096]{1,0:T(8,128)(2,1)S(1)} %slice.17) | data formatting | bytes 524288 | tf_op jit(solution)/shard_map/reshape | solution.py:108
  87.8 0.9 constant_dynamic-slice_fusion
  88.8 0.7 sub.14.ids_ref
  89.5 5.5 %all-to-all-done = bf16[32,64,768]{2,1,0:T(8,128)(2,1)S(1)} async-done(((bf16[32,64,768]{2,1,0:T(8,128)(2,1)}), bf16[32,64,768]{2,1,0:T(8,128)(2,1)S(1)}, u32[]{:S(2)}, u32[]{:S(2)}) %all-to-all-start) | async-done | bytes 3145760 | tf_op jit(solution)/shard_map/all_to_all | solution.py:100
  95.0 16.5 %shard_map.85 = (f32[2048,768]{1,0:T(8,128)}, f32[2048,1]{1,0:T(8,128)}, f32[32,1,32]{2,1,0:T(1,128)}) custom-call(s32[1,2048]{1,0:T(1,128)} %sub.14.ids_ref, bf16[2048,768]{1,0:T(8,128)(2,1)S(1)} %bitcast.15, f32[2048,768]{1,0:T(8,128)} %cent_ref.1, f32[2048,1]{1,0:T(8,128)} %copy.13.counts_ref, bf16[32,38,768]{2,1,0:T(8,128)(2,1)} %all-gather.4.cloned.1.call-done.q_ref), custom_call_target="tpu_custom_call" | custom-call | flops 9663676416 | bytes 17301504 | tf_op jit(solution)/shard_map/pallas_call | solution.py:59
  111.4 4.2 %all-to-all-start.1 = ((f32[32,1,32]{2,1,0:T(1,128)}), f32[32,1,32]{2,1,0:T(1,128)S(1)}, u32[]{:S(2)}, u32[]{:S(2)}) async-start(f32[32,1,32]{2,1,0:T(1,128)} %get-tuple-element.8), calls=%async_computation.1 | async-start | bytes 32768 | tf_op jit(solution)/shard_map/all_to_all | solution.py:122
  115.6 0.1 multiply_reduce_fusion
  115.7 2.2 %reduce = f32[2048]{0:T(1024)} reduce(f32[2048,1]{1,0:T(8,128)} %get-tuple-element.7, f32[]{:T(128)} %constant.61), dimensions={1}, to_apply=%get-tuple-element.7.reduce_sub_computation | reduce | bytes 16388 | tf_op jit(solution)/shard_map/pallas_call | solution.py:59
  117.9 4.9 %all-to-all-done.1 = f32[32,1,32]{2,1,0:T(1,128)S(1)} async-done(((f32[32,1,32]{2,1,0:T(1,128)}), f32[32,1,32]{2,1,0:T(1,128)S(1)}, u32[]{:S(2)}, u32[]{:S(2)}) %all-to-all-start.1) | async-done | bytes 4128 | tf_op jit(solution)/shard_map/all_to_all | solution.py:122
  122.8 0.1 reduce_min.9
  122.8 0.5 add_multiply_fusion
  (11 shorter events, 0.1 us)
Async XLA Ops:
  7.2 7.4 %copy-start.3 = (s32[1,32]{1,0:T(1,128)S(1)}, s32[1,32]{1,0:T(1,128)}, u32[]{:S(2)}) copy-start(s32[1,32]{1,0:T(1,128)} %param.8) | copy-start | bytes 388
  7.2 7.6 %copy-start.2 = (s32[2048]{0:T(1024)S(1)}, s32[2048]{0:T(1024)}, u32[]{:S(2)}) copy-start(s32[2048]{0:T(1024)} %param.7) | copy-start | bytes 24580
  7.2 7.7 %copy-start = (bf16[32,768]{1,0:T(8,128)(2,1)S(1)}, bf16[32,768]{1,0:T(8,128)(2,1)}, u32[]{:S(2)}) copy-start(bf16[32,768]{1,0:T(8,128)(2,1)} %param.11) | copy-start | bytes 147460
  7.2 8.3 %copy-start.1 = (f32[2048]{0:T(1024)S(1)}, f32[2048]{0:T(1024)}, u32[]{:S(2)}) copy-start(f32[2048]{0:T(1024)} %param.10) | copy-start | bytes 24580
  7.2 87.7 %all-to-all-start = ((bf16[32,64,768]{2,1,0:T(8,128)(2,1)}), bf16[32,64,768]{2,1,0:T(8,128)(2,1)S(1)}, u32[]{:S(2)}, u32[]{:S(2)}) async-start(bf16[32,64,768]{2,1,0:T(8,128)(2,1)} %bitcast.16), calls=%async_computation | async-start | bytes 6291456 | tf_op jit(solution)/shard_map/all_to_all | solution.py:100
  14.5 70.8 %all-gather.4.cloned.1.call-start = ((), (), s32[]{:S(2)}) async-start(), calls=%async_computation.2 | async-start | bytes 2027520 | tf_op jit(solution)/shard_map/all_gather | solution.py:106
  111.4 11.4 %all-to-all-start.1 = ((f32[32,1,32]{2,1,0:T(1,128)}), f32[32,1,32]{2,1,0:T(1,128)S(1)}, u32[]{:S(2)}, u32[]{:S(2)}) async-start(f32[32,1,32]{2,1,0:T(1,128)} %get-tuple-element.8), calls=%async_computation.1 | async-start | bytes 32768 | tf_op jit(solution)/shard_map/all_to_all | solution.py:122
Sparse Core Ops, SparseCore 0:
  18.8 66.4 all-gather.3
